TPU v7x, 512 devices: a whole 4x8x8 slice. The times are simulated.
512 devices in a mesh: depth: 16 (over x_hi, y), scan: 32 (over z, x_lo, core).
Axes of the slice: x: 4 (x_hi: 2, x_lo: 2; x = x_hi * 2 + x_lo), y: 8, z: 8, core: 2. Of those that a mesh axis runs over, the one named last changes fastest.
Arguments:
- object_slice: bfloat16 [2, 4, 512, 2048], P(None, None, 'depth', 'scan'), may hold values from -4 to 4
- probe_field: bfloat16 [2, 512, 512], replicated, may hold values from -2 to 2
- offsets: int32 [64, 2], replicated, may hold values from 0 to 1536
- assignment: int32 [64], P('scan'), may hold values from 0 to 63, each once
- intensities: float32 [64, 512, 512], P('scan', 'depth'), may hold values from 0 to 3
Outputs:
- object_grad: float32 [2, 4, 512, 2048], P(None, None, 'depth', 'scan')
- probe_grad: float32 [2, 512, 512], P(None, 'depth')
Inputs may be any that keep to these rules, and one draw needn't show every extreme that they name: `offsets`: each window lies inside the object window. `assignment`: every position stands in exactly one slot; slots s * 2 to s * 2 + 1 lie on index s of scan.
All inputs are finite; a program needn't handle non-finite values.
Results may differ from a plain program's by a relative error of at most 0.0003.
Values may be sent and summed in bfloat16 or wider, within the bound.
No kernel may reach another device: no remote copies, remote signals or barrier semaphores. Data moves between devices by JAX's collectives and lax.ppermute only.
A program may use at most 64 MiB of HBM per device.

v0:
```python
import math

import jax
import jax.numpy as jnp
from jax import lax
from jax.sharding import PartitionSpec as P

fresnel_scale = 4


def from_behind(block, axis, distance):
    devices = range(lax.axis_size(axis))
    route = [((i - distance) % len(devices), i) for i in devices]
    return lax.ppermute(block, axis, route)


def dft_table(size):
    index = jnp.arange(size, dtype=jnp.int32)
    turns = index[:, None] * index[None, :] % size
    angle = 2.0 * math.pi / size * turns.astype(jnp.float32)
    norm = 1.0 / math.sqrt(size)
    return (jnp.cos(angle) * norm, -jnp.sin(angle) * norm)


def chirp_phase(index, size):
    centred = index - size // 2
    period = 2 * fresnel_scale * size
    phase = centred * centred % period
    angle = math.pi / (fresnel_scale * size) * phase.astype(jnp.float32)
    return (jnp.cos(angle), jnp.sin(angle))


def contract(form, left_side, right_side):
    return jnp.einsum(
        form,
        left_side,
        right_side,
        precision=lax.Precision.HIGHEST,
        preferred_element_type=jnp.float32,
    )


def complex_mix(form, left_re, left_im, right_re, right_im):
    real_part = contract(form, left_re, right_re) - contract(form, left_im, right_im)
    imag_part = contract(form, left_re, right_im) + contract(form, left_im, right_re)
    return (real_part, imag_part)


def on_device(object_slice, probe_field, offsets, assignment, intensities):
    depth_count = lax.axis_size("depth")
    depth_index = lax.axis_index("depth")
    rows_dev = object_slice.shape[2]
    cycles = object_slice.shape[1]
    patch_side = probe_field.shape[2]
    pos_count = assignment.shape[0]
    total_pos = pos_count * lax.axis_size("scan")
    band_rows = lax.all_gather(object_slice, "scan", axis=3, tiled=True)
    full_width = band_rows.shape[3]
    flat_band = band_rows.reshape(2, cycles * rows_dev, full_width)
    position = offsets[assignment]
    top_row = position[:, 0]
    left_col = position[:, 1]
    table_re, table_im = dft_table(patch_side)
    row_ids = jnp.arange(rows_dev, dtype=jnp.int32)
    col_ids = jnp.arange(patch_side, dtype=jnp.int32)
    col_cos, col_sin = chirp_phase(col_ids, patch_side)
    zero_start = jnp.int32(0)

    def cut_tile(cycle_row, column):
        return lax.dynamic_slice(
            flat_band, (zero_start, cycle_row * rows_dev, column), (2, rows_dev, patch_side)
        )

    block_first = top_row // rows_dev
    offset_in = top_row % rows_dev
    first_block = block_first + (depth_index - block_first) % depth_count
    first_cycle = first_block // depth_count
    second_cycle = jnp.minimum(first_cycle + 1, cycles - 1)
    pair_tiles = jnp.stack(
        [jax.vmap(cut_tile)(first_cycle, left_col), jax.vmap(cut_tile)(second_cycle, left_col)], 1
    )
    levels = depth_count.bit_length() - 1
    amount = (depth_count - block_first % depth_count) % depth_count
    for level in range(levels):
        moved = from_behind(pair_tiles, "depth", 1 << level)
        taken = amount >> level & 1 == 1
        pair_tiles = jnp.where(taken[:, None, None, None, None], moved, pair_tiles)
    first_tile = pair_tiles[:, 0]
    outgoing = jnp.where(depth_index == 0, pair_tiles[:, 1], first_tile)
    following = from_behind(outgoing, "depth", depth_count - 1)
    stacked = jnp.concatenate([first_tile, following], 2)

    def take_rows(tile_pair, corner_row):
        return lax.dynamic_slice_in_dim(tile_pair, corner_row, rows_dev, 1)

    patch = jax.vmap(take_rows)(stacked, offset_in)
    patch_rows = jnp.broadcast_to(depth_index * rows_dev + row_ids[None, :], (pos_count, rows_dev))
    probe_rows = lax.dynamic_slice_in_dim(probe_field, depth_index * rows_dev, rows_dev, 1)[None]
    row_cos, row_sin = chirp_phase(patch_rows, patch_side)
    chirp_re = (
        row_cos[:, :, None] * col_cos[None, None, :] - row_sin[:, :, None] * col_sin[None, None, :]
    )
    chirp_im = (
        row_sin[:, :, None] * col_cos[None, None, :] + row_cos[:, :, None] * col_sin[None, None, :]
    )
    obj_re = patch[:, 0].astype(jnp.float32)
    obj_im = patch[:, 1].astype(jnp.float32)
    probe_re = probe_rows[:, 0].astype(jnp.float32)
    probe_im = probe_rows[:, 1].astype(jnp.float32)
    wave_re = probe_re * obj_re - probe_im * obj_im
    wave_im = probe_re * obj_im + probe_im * obj_re
    psi_re = wave_re * chirp_re - wave_im * chirp_im
    psi_im = wave_re * chirp_im + wave_im * chirp_re
    half_re, half_im = complex_mix("vk,pjk->pvj", table_re, table_im, psi_re, psi_im)
    half_re, half_im = (
        lax.all_to_all(half_re, "depth", split_axis=1, concat_axis=2, tiled=True),
        lax.all_to_all(half_im, "depth", split_axis=1, concat_axis=2, tiled=True),
    )
    far_re, far_im = complex_mix("pvj,ju->pvu", half_re, half_im, table_re, table_im)
    excess = far_re * far_re + far_im * far_im - intensities
    resid_re = excess * far_re
    resid_im = excess * far_im
    mid_re, mid_im = complex_mix("pvu,uj->pvj", resid_re, resid_im, table_re, -table_im)
    mid_re, mid_im = (
        lax.all_to_all(mid_re, "depth", split_axis=2, concat_axis=1, tiled=True),
        lax.all_to_all(mid_im, "depth", split_axis=2, concat_axis=1, tiled=True),
    )
    back_re, back_im = complex_mix("vk,pvj->pjk", table_re, -table_im, mid_re, mid_im)
    grad_re = back_re * chirp_re + back_im * chirp_im
    grad_im = back_im * chirp_re - back_re * chirp_im
    contrib = jnp.stack(
        [probe_re * grad_re + probe_im * grad_im, probe_re * grad_im - probe_im * grad_re], 1
    )
    term_re = obj_re * grad_re + obj_im * grad_im
    term_im = obj_re * grad_im - obj_im * grad_re
    grad_band = jnp.zeros((2, cycles * rows_dev, full_width), jnp.float32)

    def add_tile(band_now, tile_value, cycle_row, column):
        corner = (zero_start, cycle_row * rows_dev, column)
        current = lax.dynamic_slice(band_now, corner, (2, rows_dev, patch_side))
        return lax.dynamic_update_slice(band_now, current + tile_value, corner)

    empty_window = jnp.zeros((pos_count, 2, 2 * rows_dev, patch_side), jnp.float32)

    def place_rows(window_zero, tile_rows, corner_row):
        return lax.dynamic_update_slice_in_dim(window_zero, tile_rows, corner_row, 1)

    placed = jax.vmap(place_rows)(empty_window, contrib, offset_in)
    head_part = placed[:, :, :rows_dev]
    tail_part = placed[:, :, rows_dev:]
    returned = from_behind(tail_part, "depth", 1)
    is_first = depth_index == 0
    head_part = jnp.where(is_first, head_part, head_part + returned)
    second_part = jnp.where(is_first, returned, jnp.zeros_like(returned))
    grad_pair = jnp.stack([head_part, second_part], 1)
    amount_back = block_first % depth_count
    for level in range(levels):
        moved_back = from_behind(grad_pair, "depth", 1 << level)
        taken_back = amount_back >> level & 1 == 1
        grad_pair = jnp.where(taken_back[:, None, None, None, None], moved_back, grad_pair)
    for slot_index in range(pos_count):
        grad_band = add_tile(
            grad_band, grad_pair[slot_index, 0], first_cycle[slot_index], left_col[slot_index]
        )
        grad_band = add_tile(
            grad_band, grad_pair[slot_index, 1], second_cycle[slot_index], left_col[slot_index]
        )
    probe_sum = jnp.stack([jnp.sum(term_re, 0), jnp.sum(term_im, 0)])
    probe_grad = lax.psum(probe_sum, "scan")
    object_grad = lax.psum_scatter(
        grad_band.reshape(2, cycles, rows_dev, full_width), "scan", scatter_dimension=3, tiled=True
    )
    return (object_grad, probe_grad * total_pos ** (-0.5))


def solution(mesh):
    return jax.shard_map(
        on_device,
        mesh=mesh,
        in_specs=(P(None, None, "depth", "scan"), P(), P(), P("scan"), P("scan", "depth", None)),
        out_specs=(P(None, None, "depth", "scan"), P(None, "depth", None)),
        check_vma=False,
    )
```

profile of v0, /device:TPU:7, one launch (start us, length us, event | category | flops | bytes accessed | tf_op | source)
XLA Modules:
  0.0 741.1 jit_solution(7698439106445803496)
XLA Ops:
  11.9 73.0 %all-gather.2.cloned.1.call-done = bf16[2,4,32,2048]{2,1,0,3:T(4,128)(2,1)} async-done(((bf16[2,4,32,64]{2,1,0,3:T(4,128)(2,1)}), bf16[2,4,32,2048]{2,1,0,3:T(4,128)(2,1)}) %all-gather.2.cloned.1.call-update) | async-done | bytes 1048592 | tf_op jit(solution)/shard_map/all_gather | solution.py:57
  84.9 5.5 copy.64
  102.4 10.0 %collective-permute-done = bf16[2,2,2,32,512]{4,2,0,3,1:T(2,128)(2,1)S(1)} collective-permute-done((bf16[2,2,2,32,512]{4,2,0,3,1:T(2,128)(2,1)S(1)}, bf16[2,2,2,32,512]{4,2,0,3,1:T(2,128)(2,1)S(1)}, u32[]{:S(2)}, u32[]{:S(2)}) %collective-permute-start) | collective-permute-done | bytes 262176 | tf_op jit(solution)/shard_map/ppermute | solution.py:14
  114.9 15.1 %collective-permute-done.1 = bf16[2,2,2,32,512]{4,2,0,3,1:T(2,128)(2,1)S(1)} collective-permute-done((bf16[2,2,2,32,512]{4,2,0,3,1:T(2,128)(2,1)S(1)}, bf16[2,2,2,32,512]{4,2,0,3,1:T(2,128)(2,1)S(1)}, u32[]{:S(2)}, u32[]{:S(2)}) %collective-permute-start.1) | collective-permute-done | bytes 262176 | tf_op jit(solution)/shard_map/ppermute | solution.py:14
  134.3 15.0 %collective-permute-done.2 = bf16[2,2,2,32,512]{4,2,0,3,1:T(2,128)(2,1)S(1)} collective-permute-done((bf16[2,2,2,32,512]{4,2,0,3,1:T(2,128)(2,1)S(1)}, bf16[2,2,2,32,512]{4,2,0,3,1:T(2,128)(2,1)S(1)}, u32[]{:S(2)}, u32[]{:S(2)}) %collective-permute-start.2) | collective-permute-done | bytes 262176 | tf_op jit(solution)/shard_map/ppermute | solution.py:14
  154.0 5.7 collective-permute-done.3
  177.3 5.2 fusion.1
  184.0 7.7 %all-to-all-start = ((f32[16,1,2048]{2,1,0:T(1,128)}), f32[16,1,2048]{2,1,0:T(1,128)S(1)}, u32[]{:S(2)}, u32[]{:S(2)}) async-start(f32[16,1,2048]{2,1,0:T(1,128)} %reshape.369), calls=%async_computation | async-start | bytes 262144 | tf_op jit(solution)/shard_map/all_to_all | solution.py:116
  198.6 9.1 %all-to-all-start.1 = ((f32[16,1,2048]{2,1,0:T(1,128)}), f32[16,1,2048]{2,1,0:T(1,128)S(1)}, u32[]{:S(2)}, u32[]{:S(2)}) async-start(f32[16,1,2048]{2,1,0:T(1,128)} %reshape.371), calls=%async_computation.1 | async-start | bytes 262144 | tf_op jit(solution)/shard_map/all_to_all | solution.py:117
  247.3 9.1 %all-to-all-start.2 = ((f32[16,1,2048]{2,1,0:T(1,128)}), f32[16,1,2048]{2,1,0:T(1,128)S(1)}, u32[]{:S(2)}, u32[]{:S(2)}) async-start(f32[16,1,2048]{2,1,0:T(1,128)} %reshape.375), calls=%async_computation.2 | async-start | bytes 262144 | tf_op jit(solution)/shard_map/all_to_all | solution.py:125
  263.0 8.6 %all-to-all-start.3 = ((f32[16,1,2048]{2,1,0:T(1,128)}), f32[16,1,2048]{2,1,0:T(1,128)S(1)}, u32[]{:S(2)}, u32[]{:S(2)}) async-start(f32[16,1,2048]{2,1,0:T(1,128)} %reshape.373), calls=%async_computation.3 | async-start | bytes 262144 | tf_op jit(solution)/shard_map/all_to_all | solution.py:126
  295.3 14.5 %while.5 = (s32[]{:T(128)}, f32[2,2,64,512]{3,1,0,2:T(2,128)S(1)}, s32[2,4]{1,0:T(2,128)S(1)}, f32[2,2,32,512]{3,2,0,1:T(8,128)S(1)}, s32[]{:T(128)}, /*index=5*/s32[4]{0:T(128)S(1)}) while((s32[]{:T(128)}, f32[2,2,64,512]{3,1,0,2:T(2,128)S(1)}, s32[2,4]{1,0:T(2,128)S(1)}, f32[2,2,32,512]{3,2,0,1:T(8,128)S(1)}, s32[]{:T(128)}, ...), condition=%wide.while_cond.2, body=%wide.while_body.2.sunk | while | flops 32797 | bytes 917703 | solution.py:146
  312.9 7.6 %collective-permute-done.5 = f32[2,2,32,512]{3,1,0,2:T(2,128)S(1)} collective-permute-done((f32[2,2,32,512]{3,1,0,2:T(2,128)S(1)}, f32[2,2,32,512]{3,1,0,2:T(2,128)S(1)}, u32[]{:S(2)}, u32[]{:S(2)}) %collective-permute-start.5) | collective-permute-done | bytes 262176 | tf_op jit(solution)/shard_map/ppermute | solution.py:14
  323.2 11.4 %collective-permute-done.6 = f32[2,2,2,32,512]{4,2,0,3,1:T(2,128)S(1)} collective-permute-done((f32[2,2,2,32,512]{4,2,0,3,1:T(2,128)S(1)}, f32[2,2,2,32,512]{4,2,0,3,1:T(2,128)S(1)}, u32[]{:S(2)}, u32[]{:S(2)}) %collective-permute-start.6) | collective-permute-done | bytes 524320 | tf_op jit(solution)/shard_map/ppermute | solution.py:14
  336.9 22.0 %collective-permute-done.7 = f32[2,2,2,32,512]{4,2,0,3,1:T(2,128)S(1)} collective-permute-done((f32[2,2,2,32,512]{4,2,0,3,1:T(2,128)S(1)}, f32[2,2,2,32,512]{4,2,0,3,1:T(2,128)S(1)}, u32[]{:S(2)}, u32[]{:S(2)}) %collective-permute-start.7) | collective-permute-done | bytes 524320 | tf_op jit(solution)/shard_map/ppermute | solution.py:14
  361.3 23.8 %collective-permute-done.8 = f32[2,2,2,32,512]{4,2,0,3,1:T(2,128)S(1)} collective-permute-done((f32[2,2,2,32,512]{4,2,0,3,1:T(2,128)S(1)}, f32[2,2,2,32,512]{4,2,0,3,1:T(2,128)S(1)}, u32[]{:S(2)}, u32[]{:S(2)}) %collective-permute-start.8) | collective-permute-done | bytes 524320 | tf_op jit(solution)/shard_map/ppermute | solution.py:14
  399.8 6.1 dynamic_update_slice.12
  407.0 6.1 dynamic_update_slice.13
  414.3 6.2 dynamic_update_slice.14
  421.6 6.2 dynamic_update_slice.15
  427.8 6.1 copy.84
  434.0 8.6 %reshape.365 = f32[2048,256]{1,0:T(8,128)} reshape(f32[2048,2,4,32]{3,2,1,0:T(4,128)} %bitcast.195) | data formatting | bytes 4194304
  442.6 170.4 %all-reduce.2.cloned.1.call-done = f32[2,32,512]{2,1,0:T(8,128)} async-done(((f32[2,32,512]{2,1,0:T(8,128)}), f32[2,32,512]{2,1,0:T(8,128)}) %all-reduce.2.cloned.1.call-update) | async-done | bytes 131088 | tf_op jit(solution)/shard_map/psum | solution.py:169
  614.5 117.8 %reduce-scatter.4.cloned.1.call-done = f32[64,256]{1,0:T(8,128)} async-done(((f32[2048,256]{1,0:T(8,128)}), f32[64,256]{1,0:T(8,128)}) %reduce-scatter.4.cloned.1.call-update) | async-done | bytes 65552
  (155 shorter events, 171.7 us)
Async XLA Ops:
  7.2 107.7 %copy-start = (bf16[2,512,512]{2,1,0:T(8,128)(2,1)S(1)}, bf16[2,512,512]{2,1,0:T(8,128)(2,1)}, u32[]{:S(2)}) copy-start(bf16[2,512,512]{2,1,0:T(8,128)(2,1)} %param.6) | copy-start | bytes 3145732
  7.2 77.7 %all-gather.2.cloned.1.call-start = ((), (), s32[]{:S(2)}) async-start(), calls=%async_computation.5 | async-start | bytes 4325376 | tf_op jit(solution)/shard_map/all_gather | solution.py:57
  99.3 13.1 %collective-permute-start = (bf16[2,2,2,32,512]{4,2,0,3,1:T(2,128)(2,1)S(1)}, bf16[2,2,2,32,512]{4,2,0,3,1:T(2,128)(2,1)S(1)}, u32[]{:S(2)}, u32[]{:S(2)}) collective-permute-start(bf16[2,2,2,32,512]{4,2,0,3,1:T(2,128)(2,1)S(1)} %pad_maximum_fusion.1), channel_id=1, source_target_pairs={{480,0},{0,32},{32,64},{64,96},{96,128},{128,160},{160,192},{192,2... | collective-permute-start | bytes 786440 | tf_op jit(solution)/shard_map/ppermute | solution.py:14
  112.9 17.1 %collective-permute-start.1 = (bf16[2,2,2,32,512]{4,2,0,3,1:T(2,128)(2,1)S(1)}, bf16[2,2,2,32,512]{4,2,0,3,1:T(2,128)(2,1)S(1)}, u32[]{:S(2)}, u32[]{:S(2)}) collective-permute-start(bf16[2,2,2,32,512]{4,2,0,3,1:T(2,128)(2,1)S(1)} %broadcast_select_fusion.4), channel_id=1, source_target_pairs={{448,0},{480,32},{0,64},{32,96},{64,128},{96,160},{128,192},{160,2... | collective-permute-start | bytes 786440 | tf_op jit(solution)/shard_map/ppermute | solution.py:14
  130.6 18.8 %collective-permute-start.2 = (bf16[2,2,2,32,512]{4,2,0,3,1:T(2,128)(2,1)S(1)}, bf16[2,2,2,32,512]{4,2,0,3,1:T(2,128)(2,1)S(1)}, u32[]{:S(2)}, u32[]{:S(2)}) collective-permute-start(bf16[2,2,2,32,512]{4,2,0,3,1:T(2,128)(2,1)S(1)} %broadcast_select_fusion.5), channel_id=1, source_target_pairs={{384,0},{416,32},{448,64},{480,96},{0,128},{32,160},{64,192},{96,2... | collective-permute-start | bytes 786440 | tf_op jit(solution)/shard_map/ppermute | solution.py:14
  149.7 10.0 %collective-permute-start.3 = (bf16[2,2,2,32,512]{4,2,0,3,1:T(2,128)(2,1)S(1)}, bf16[2,2,2,32,512]{4,2,0,3,1:T(2,128)(2,1)S(1)}, u32[]{:S(2)}, u32[]{:S(2)}) collective-permute-start(bf16[2,2,2,32,512]{4,2,0,3,1:T(2,128)(2,1)S(1)} %broadcast_select_fusion.6), channel_id=1, source_target_pairs={{256,0},{288,32},{320,64},{352,96},{384,128},{416,160},{448,192},{... | collective-permute-start | bytes 786440 | tf_op jit(solution)/shard_map/ppermute | solution.py:14
  160.2 5.7 collective-permute-start.4
  184.0 14.6 %all-to-all-start = ((f32[16,1,2048]{2,1,0:T(1,128)}), f32[16,1,2048]{2,1,0:T(1,128)S(1)}, u32[]{:S(2)}, u32[]{:S(2)}) async-start(f32[16,1,2048]{2,1,0:T(1,128)} %reshape.369), calls=%async_computation | async-start | bytes 262144 | tf_op jit(solution)/shard_map/all_to_all | solution.py:116
  198.6 21.2 %all-to-all-start.1 = ((f32[16,1,2048]{2,1,0:T(1,128)}), f32[16,1,2048]{2,1,0:T(1,128)S(1)}, u32[]{:S(2)}, u32[]{:S(2)}) async-start(f32[16,1,2048]{2,1,0:T(1,128)} %reshape.371), calls=%async_computation.1 | async-start | bytes 262144 | tf_op jit(solution)/shard_map/all_to_all | solution.py:117
  226.4 5.0 copy-start.3
  247.3 15.8 %all-to-all-start.2 = ((f32[16,1,2048]{2,1,0:T(1,128)}), f32[16,1,2048]{2,1,0:T(1,128)S(1)}, u32[]{:S(2)}, u32[]{:S(2)}) async-start(f32[16,1,2048]{2,1,0:T(1,128)} %reshape.375), calls=%async_computation.2 | async-start | bytes 262144 | tf_op jit(solution)/shard_map/all_to_all | solution.py:125
  263.0 15.6 %all-to-all-start.3 = ((f32[16,1,2048]{2,1,0:T(1,128)}), f32[16,1,2048]{2,1,0:T(1,128)S(1)}, u32[]{:S(2)}, u32[]{:S(2)}) async-start(f32[16,1,2048]{2,1,0:T(1,128)} %reshape.373), calls=%async_computation.3 | async-start | bytes 262144 | tf_op jit(solution)/shard_map/all_to_all | solution.py:126
  271.6 341.4 %all-reduce.2.cloned.1.call-start = ((), (), s32[]{:S(2)}) async-start(), calls=%async_computation.6 | async-start | bytes 262144 | tf_op jit(solution)/shard_map/psum | solution.py:169
  290.2 5.1 copy-start.2
  309.8 10.7 %collective-permute-start.5 = (f32[2,2,32,512]{3,1,0,2:T(2,128)S(1)}, f32[2,2,32,512]{3,1,0,2:T(2,128)S(1)}, u32[]{:S(2)}, u32[]{:S(2)}) collective-permute-start(f32[2,2,32,512]{3,1,0,2:T(2,128)S(1)} %slice.75), channel_id=1, source_target_pairs={{480,0},{0,32},{32,64},{64,96},{96,128},{128,160},{160,192},{192,2... | collective-permute-start | bytes 786440 | tf_op jit(solution)/shard_map/ppermute | solution.py:14
  321.0 13.5 %collective-permute-start.6 = (f32[2,2,2,32,512]{4,2,0,3,1:T(2,128)S(1)}, f32[2,2,2,32,512]{4,2,0,3,1:T(2,128)S(1)}, u32[]{:S(2)}, u32[]{:S(2)}) collective-permute-start(f32[2,2,2,32,512]{4,2,0,3,1:T(2,128)S(1)} %pad_maximum_fusion), channel_id=1, source_target_pairs={{480,0},{0,32},{32,64},{64,96},{96,128},{128,160},{160,192},{192,2... | collective-permute-start | bytes 1572872 | tf_op jit(solution)/shard_map/ppermute | solution.py:14
  334.9 23.9 %collective-permute-start.7 = (f32[2,2,2,32,512]{4,2,0,3,1:T(2,128)S(1)}, f32[2,2,2,32,512]{4,2,0,3,1:T(2,128)S(1)}, u32[]{:S(2)}, u32[]{:S(2)}) collective-permute-start(f32[2,2,2,32,512]{4,2,0,3,1:T(2,128)S(1)} %broadcast_select_fusion), channel_id=1, source_target_pairs={{448,0},{480,32},{0,64},{32,96},{64,128},{96,160},{128,192},{160,2... | collective-permute-start | bytes 1572872 | tf_op jit(solution)/shard_map/ppermute | solution.py:14
  359.3 25.7 %collective-permute-start.8 = (f32[2,2,2,32,512]{4,2,0,3,1:T(2,128)S(1)}, f32[2,2,2,32,512]{4,2,0,3,1:T(2,128)S(1)}, u32[]{:S(2)}, u32[]{:S(2)}) collective-permute-start(f32[2,2,2,32,512]{4,2,0,3,1:T(2,128)S(1)} %broadcast_select_fusion.1), channel_id=1, source_target_pairs={{384,0},{416,32},{448,64},{480,96},{0,128},{32,160},{64,192},{96,2... | collective-permute-start | bytes 1572872 | tf_op jit(solution)/shard_map/ppermute | solution.py:14
  385.4 12.2 %collective-permute-start.9 = (f32[2,2,2,32,512]{4,2,0,3,1:T(2,128)S(1)}, f32[2,2,2,32,512]{4,2,0,3,1:T(2,128)S(1)}, u32[]{:S(2)}, u32[]{:S(2)}) collective-permute-start(f32[2,2,2,32,512]{4,2,0,3,1:T(2,128)S(1)} %broadcast_select_fusion.2), channel_id=1, source_target_pairs={{256,0},{288,32},{320,64},{352,96},{384,128},{416,160},{448,192},{... | collective-permute-start | bytes 1572872 | tf_op jit(solution)/shard_map/ppermute | solution.py:14
  395.6 336.7 %reduce-scatter.4.cloned.1.call-start = ((), (), s32[]{:S(2)}) async-start(), calls=%async_computation.7 | async-start | bytes 2162688
  397.9 0.8 copy-start.1
Sparse Core Ops, SparseCore 0:
  10.7 74.1 all-gather.1
  395.7 217.1 all-reduce.1
  615.8 116.4 reduce-scatter.3
where the time goes:
time: 754 us; the launch traced here: 741 us
  waiting for transfers between devices  478 us (63%)
  local copies, waits for them, and re-layouts  79.3 us (11%)
  matrix products  78 us (10%)
  starting transfers between devices  60.6 us (8%)
  other arithmetic  23.6 us (3%)
  between operations  21.3 us (3%)
    psum x1, waiting for transfers between devices, on_device(): probe_grad = lax.psum(probe_sum, 'scan')  170 us
    unnamed x4, waiting for transfers between devices  118 us
    ppermute x10, waiting for transfers between devices, from_behind(): return lax.ppermute(block, axis, route)  116 us
    dot_general x16, matrix products, contract(): jnp.einsum(form, left_side, right_side, precision=lax.Precision.HIGHEST,...  78 us
    all_gather x1, waiting for transfers between devices, on_device(): band_rows = lax.all_gather(object_slice, 'scan', axis=3, tiled=True)  73 us
    unnamed x26, local copies, waits for them, and re-layouts  26.6 us
    ppermute x10, starting transfers between devices, from_behind(): return lax.ppermute(block, axis, route)  26 us
    dynamic_update_slice x4, local copies, waits for them, and re-layouts, add_tile(): return lax.dynamic_update_slice(band_now, current + tile_value, corner)  24.7 us
  transfers between devices with their start and end apart: 17, of which 15 were waited for; matrix products, arithmetic and copies ran while one was open for 11% of the time, Pallas kernels for 0%

commit v1 on v0

--- a/solution.py
+++ b/solution.py
@@ -12,6 +12,16 @@
     devices = range(lax.axis_size(axis))
     route = [((i - distance) % len(devices), i) for i in devices]
     return lax.ppermute(block, axis, route)
+
+
+def gather_blocks(block, axis):
+    count = lax.axis_size(axis)
+    spread = jnp.broadcast_to(block[None], (count,) + block.shape)
+    return lax.all_to_all(spread, axis, 0, 0, tiled=True)
+
+
+def sum_blocks(chunks, axis):
+    return jnp.sum(lax.all_to_all(chunks, axis, 0, 0, tiled=True), 0)
 
 
 def dft_table(size):
@@ -54,7 +64,11 @@
     patch_side = probe_field.shape[2]
     pos_count = assignment.shape[0]
     total_pos = pos_count * lax.axis_size("scan")
-    band_rows = lax.all_gather(object_slice, "scan", axis=3, tiled=True)
+    scan_count = lax.axis_size("scan")
+    gathered = gather_blocks(object_slice, "scan")
+    band_rows = jnp.moveaxis(gathered, 0, 3).reshape(
+        object_slice.shape[:3] + (scan_count * object_slice.shape[3],)
+    )
     full_width = band_rows.shape[3]
     flat_band = band_rows.reshape(2, cycles * rows_dev, full_width)
     position = offsets[assignment]
@@ -112,18 +126,16 @@
     psi_re = wave_re * chirp_re - wave_im * chirp_im
     psi_im = wave_re * chirp_im + wave_im * chirp_re
     half_re, half_im = complex_mix("vk,pjk->pvj", table_re, table_im, psi_re, psi_im)
-    half_re, half_im = (
-        lax.all_to_all(half_re, "depth", split_axis=1, concat_axis=2, tiled=True),
-        lax.all_to_all(half_im, "depth", split_axis=1, concat_axis=2, tiled=True),
+    half_re, half_im = lax.all_to_all(
+        jnp.stack([half_re, half_im]), "depth", split_axis=2, concat_axis=3, tiled=True
     )
     far_re, far_im = complex_mix("pvj,ju->pvu", half_re, half_im, table_re, table_im)
     excess = far_re * far_re + far_im * far_im - intensities
     resid_re = excess * far_re
     resid_im = excess * far_im
     mid_re, mid_im = complex_mix("pvu,uj->pvj", resid_re, resid_im, table_re, -table_im)
-    mid_re, mid_im = (
-        lax.all_to_all(mid_re, "depth", split_axis=2, concat_axis=1, tiled=True),
-        lax.all_to_all(mid_im, "depth", split_axis=2, concat_axis=1, tiled=True),
+    mid_re, mid_im = lax.all_to_all(
+        jnp.stack([mid_re, mid_im]), "depth", split_axis=3, concat_axis=2, tiled=True
     )
     back_re, back_im = complex_mix("vk,pvj->pjk", table_re, -table_im, mid_re, mid_im)
     grad_re = back_re * chirp_re + back_im * chirp_im
@@ -166,9 +178,11 @@
             grad_band, grad_pair[slot_index, 1], second_cycle[slot_index], left_col[slot_index]
         )
     probe_sum = jnp.stack([jnp.sum(term_re, 0), jnp.sum(term_im, 0)])
-    probe_grad = lax.psum(probe_sum, "scan")
-    object_grad = lax.psum_scatter(
-        grad_band.reshape(2, cycles, rows_dev, full_width), "scan", scatter_dimension=3, tiled=True
+    probe_part = sum_blocks(probe_sum.reshape(scan_count, -1), "scan")
+    probe_grad = gather_blocks(probe_part, "scan").reshape(probe_sum.shape)
+    col_chunks = grad_band.reshape(2, cycles * rows_dev, scan_count, full_width // scan_count)
+    object_grad = sum_blocks(jnp.moveaxis(col_chunks, 2, 0), "scan").reshape(
+        2, cycles, rows_dev, full_width // scan_count
     )
     return (object_grad, probe_grad * total_pos ** (-0.5))
 

time: 754 us -> 480 us (0.64)
  waiting for transfers between devices: 478 us -> 185 us
  starting transfers between devices: 60.6 us -> 90 us
  blocking collectives: 0 us -> 15.4 us
  between operations: 21.3 us -> 8.04 us
    psum x1 -> x0, waiting for transfers between devices: 170 us -> none  [on_device(): probe_grad = lax.psum(probe_sum, 'scan')]
    unnamed x4 -> x0, waiting for transfers between devices: 118 us -> none
    all_to_all x4 -> x5, waiting for transfers between devices: 0.92 us -> 84.1 us  [the longest x2 49.7 us: sum_blocks(): return jnp.sum(lax.all_to_all(chunks, axis, 0, 0, tiled=True), 0)]
    all_gather x1 -> x0, waiting for transfers between devices: 73 us -> none  [on_device(): band_rows = lax.all_gather(object_slice, 'scan', axis=3, tiled=True)]
    all_to_all x4 -> x5, starting transfers between devices: 34.5 us -> 52.3 us  [the longest x2 26.3 us: sum_blocks(): return jnp.sum(lax.all_to_all(chunks, axis, 0, 0, tiled=True), 0)]
    all_to_all x0 -> x1, blocking collectives: none -> 15.4 us  [on_device(): lax.all_to_all(jnp.stack([half_re, half_im]), 'depth', split_axis=2, conc...]
    ppermute x10, waiting for transfers between devices: 116 us -> 101 us  [from_behind(): return lax.ppermute(block, axis, route)]
    unnamed x26 -> x25, local copies, waits for them, and re-layouts: 26.6 us -> 11.7 us
  transfers between devices with their start and end apart: 17 -> 15, of which waited for: 15 -> 13; matrix products, arithmetic and copies ran while one was open for 11% -> 8% of each run, Pallas kernels for 0% -> 0%
where the time goes in v1:
time: 480 us; the launch traced here: 473 us
  waiting for transfers between devices  185 us (39%)
  starting transfers between devices  90 us (19%)
  matrix products  78.3 us (16%)
  local copies, waits for them, and re-layouts  76.1 us (16%)
  other arithmetic  19.8 us (4%)
  blocking collectives  15.4 us (3%)
  between operations  8.04 us (2%)
    ppermute x10, waiting for transfers between devices, from_behind(): return lax.ppermute(block, axis, route)  101 us
    dot_general x16, matrix products, contract(): jnp.einsum(form, left_side, right_side, precision=lax.Precision.HIGHEST,...  78.3 us
    all_to_all x2, waiting for transfers between devices, sum_blocks(): return jnp.sum(lax.all_to_all(chunks, axis, 0, 0, tiled=True), 0)  49.7 us
    ppermute x10, starting transfers between devices, from_behind(): return lax.ppermute(block, axis, route)  37.7 us
    all_to_all x2, waiting for transfers between devices, gather_blocks(): return lax.all_to_all(spread, axis, 0, 0, tiled=True)  27.3 us
    dynamic_update_slice x5, local copies, waits for them, and re-layouts, add_tile(): return lax.dynamic_update_slice(band_now, current + tile_value, corner)  27.2 us
    all_to_all x2, starting transfers between devices, sum_blocks(): return jnp.sum(lax.all_to_all(chunks, axis, 0, 0, tiled=True), 0)  26.3 us
    all_to_all x2, starting transfers between devices, gather_blocks(): return lax.all_to_all(spread, axis, 0, 0, tiled=True)  19.9 us
  transfers between devices with their start and end apart: 15, of which 13 were waited for; matrix products, arithmetic and copies ran while one was open for 8% of the time, Pallas kernels for 0%

profile of v1, /device:TPU:7, one launch (start us, length us, event | category | flops | bytes accessed | tf_op | source)
XLA Modules:
  0.0 472.5 jit_solution(11376587112439917101)
XLA Ops:
  4.4 12.3 %all-to-all-start = ((bf16[32,2,8192]{2,1,0:T(2,128)(2,1)}), bf16[32,2,8192]{2,1,0:T(2,128)(2,1)}, u32[]{:S(2)}, u32[]{:S(2)}) async-start(bf16[32,2,8192]{2,1,0:T(2,128)(2,1)} %reshape.391), calls=%async_computation | async-start | bytes 2097152 | tf_op jit(solution)/shard_map/all_to_all | solution.py:20
  17.7 27.3 %all-to-all-done = bf16[32,2,8192]{2,1,0:T(2,128)(2,1)} async-done(((bf16[32,2,8192]{2,1,0:T(2,128)(2,1)}), bf16[32,2,8192]{2,1,0:T(2,128)(2,1)}, u32[]{:S(2)}, u32[]{:S(2)}) %all-to-all-start) | async-done | bytes 1048608 | tf_op jit(solution)/shard_map/all_to_all | solution.py:20
  67.1 9.1 %collective-permute-done = bf16[2,2,2,32,512]{4,2,0,3,1:T(2,128)(2,1)S(1)} collective-permute-done((bf16[2,2,2,32,512]{4,2,0,3,1:T(2,128)(2,1)S(1)}, bf16[2,2,2,32,512]{4,2,0,3,1:T(2,128)(2,1)S(1)}, u32[]{:S(2)}, u32[]{:S(2)}) %collective-permute-start) | collective-permute-done | bytes 262176 | tf_op jit(solution)/shard_map/ppermute | solution.py:14
  78.7 16.1 %collective-permute-done.1 = bf16[2,2,2,32,512]{4,2,0,3,1:T(2,128)(2,1)S(1)} collective-permute-done((bf16[2,2,2,32,512]{4,2,0,3,1:T(2,128)(2,1)S(1)}, bf16[2,2,2,32,512]{4,2,0,3,1:T(2,128)(2,1)S(1)}, u32[]{:S(2)}, u32[]{:S(2)}) %collective-permute-start.1) | collective-permute-done | bytes 262176 | tf_op jit(solution)/shard_map/ppermute | solution.py:14
  98.8 14.4 %collective-permute-done.2 = bf16[2,2,2,32,512]{4,2,0,3,1:T(2,128)(2,1)S(1)} collective-permute-done((bf16[2,2,2,32,512]{4,2,0,3,1:T(2,128)(2,1)S(1)}, bf16[2,2,2,32,512]{4,2,0,3,1:T(2,128)(2,1)S(1)}, u32[]{:S(2)}, u32[]{:S(2)}) %collective-permute-start.2) | collective-permute-done | bytes 262176 | tf_op jit(solution)/shard_map/ppermute | solution.py:14
  118.0 5.5 %collective-permute-done.3 = bf16[2,2,2,32,512]{4,2,0,3,1:T(2,128)(2,1)S(1)} collective-permute-done((bf16[2,2,2,32,512]{4,2,0,3,1:T(2,128)(2,1)S(1)}, bf16[2,2,2,32,512]{4,2,0,3,1:T(2,128)(2,1)S(1)}, u32[]{:S(2)}, u32[]{:S(2)}) %collective-permute-start.3) | collective-permute-done | bytes 262176 | tf_op jit(solution)/shard_map/ppermute | solution.py:14
  141.0 5.2 %fusion.3 = f32[1,2,512,32]{2,3,1,0:T(8,128)S(1)} fusion(f32[2,32,512]{2,1,0:T(8,128)S(1)} %fusion.29, bf16[2,32,512]{2,1,0:T(8,128)(2,1)S(1)} %get-tuple-element.133, bf16[2,32,512]{2,1,0:T(8,128)(2,1)S(1)} %get-tuple-element.132, f32[512]{0:T(512)S(1)} %get-tuple-element.134, f32[2,32]{1,0:T(2,128)S(1)} %get-tuple-element.106, ...), kind=kOutput, calls=%fused_computation.27 | convolution fusion | flops 206110720 | bytes 528896 | tf_op jit(solution)/shard_map/vk,pjk->pvj/dot_general | solution.py:44
  153.0 15.4 %all_to_all.55 = f32[16,1,4096]{2,1,0:T(1,128)S(1)} all-to-all(f32[16,1,4096]{2,1,0:T(1,128)S(1)} %reshape.393), channel_id=1, replica_groups=mesh['depth'=16,'scan'=32] {'depth'}, dimensions={0} | all-to-all | bytes 524288 | tf_op jit(solution)/shard_map/all_to_all | solution.py:129
  213.7 6.2 %all-to-all-start.2 = ((f32[16,1,4096]{2,1,0:T(1,128)}), f32[16,1,4096]{2,1,0:T(1,128)S(1)}, u32[]{:S(2)}, u32[]{:S(2)}) async-start(f32[16,1,4096]{2,1,0:T(1,128)} %reshape.395), calls=%async_computation.2 | async-start | bytes 524288 | tf_op jit(solution)/shard_map/all_to_all | solution.py:137
  219.9 7.0 %all-to-all-done.2 = f32[16,1,4096]{2,1,0:T(1,128)S(1)} async-done(((f32[16,1,4096]{2,1,0:T(1,128)}), f32[16,1,4096]{2,1,0:T(1,128)S(1)}, u32[]{:S(2)}, u32[]{:S(2)}) %all-to-all-start.2) | async-done | bytes 262176 | tf_op jit(solution)/shard_map/all_to_all | solution.py:137
  250.0 14.7 %while.5 = (s32[]{:T(128)}, f32[2,2,64,512]{3,1,0,2:T(2,128)S(1)}, s32[2,4]{1,0:T(2,128)S(1)}, f32[2,2,32,512]{3,2,0,1:T(8,128)S(1)}, s32[]{:T(128)}, /*index=5*/s32[4]{0:T(128)S(1)}) while((s32[]{:T(128)}, f32[2,2,64,512]{3,1,0,2:T(2,128)S(1)}, s32[2,4]{1,0:T(2,128)S(1)}, f32[2,2,32,512]{3,2,0,1:T(8,128)S(1)}, s32[]{:T(128)}, ...), condition=%wide.while_cond.2, body=%wide.while_body.2.sunk | while | flops 32797 | bytes 917695 | solution.py:158
  268.9 6.6 %collective-permute-done.5 = f32[2,2,32,512]{3,1,0,2:T(2,128)S(1)} collective-permute-done((f32[2,2,32,512]{3,1,0,2:T(2,128)S(1)}, f32[2,2,32,512]{3,1,0,2:T(2,128)S(1)}, u32[]{:S(2)}, u32[]{:S(2)}) %collective-permute-start.5) | collective-permute-done | bytes 262176 | tf_op jit(solution)/shard_map/ppermute | solution.py:14
  277.9 11.6 %collective-permute-done.6 = f32[2,2,2,32,512]{4,2,0,3,1:T(2,128)S(1)} collective-permute-done((f32[2,2,2,32,512]{4,2,0,3,1:T(2,128)S(1)}, f32[2,2,2,32,512]{4,2,0,3,1:T(2,128)S(1)}, u32[]{:S(2)}, u32[]{:S(2)}) %collective-permute-start.6) | collective-permute-done | bytes 524320 | tf_op jit(solution)/shard_map/ppermute | solution.py:14
  291.8 16.6 %collective-permute-done.7 = f32[2,2,2,32,512]{4,2,0,3,1:T(2,128)S(1)} collective-permute-done((f32[2,2,2,32,512]{4,2,0,3,1:T(2,128)S(1)}, f32[2,2,2,32,512]{4,2,0,3,1:T(2,128)S(1)}, u32[]{:S(2)}, u32[]{:S(2)}) %collective-permute-start.7) | collective-permute-done | bytes 524320 | tf_op jit(solution)/shard_map/ppermute | solution.py:14
  313.8 17.6 %collective-permute-done.8 = f32[2,2,2,32,512]{4,2,0,3,1:T(2,128)S(1)} collective-permute-done((f32[2,2,2,32,512]{4,2,0,3,1:T(2,128)S(1)}, f32[2,2,2,32,512]{4,2,0,3,1:T(2,128)S(1)}, u32[]{:S(2)}, u32[]{:S(2)}) %collective-permute-start.8) | collective-permute-done | bytes 524320 | tf_op jit(solution)/shard_map/ppermute | solution.py:14
  331.7 9.7 %collective-permute-start.9 = (f32[2,2,2,32,512]{4,2,0,3,1:T(2,128)S(1)}, f32[2,2,2,32,512]{4,2,0,3,1:T(2,128)S(1)}, u32[]{:S(2)}, u32[]{:S(2)}) collective-permute-start(f32[2,2,2,32,512]{4,2,0,3,1:T(2,128)S(1)} %broadcast_select_fusion.2), channel_id=1, source_target_pairs={{256,0},{288,32},{320,64},{352,96},{384,128},{416,160},{448,192},{... | collective-permute-start | bytes 1572872 | tf_op jit(solution)/shard_map/ppermute | solution.py:14
  342.2 18.2 %all-to-all-start.4 = ((f32[32,1,1024]{2,1,0:T(1,128)}), f32[32,1,1024]{2,1,0:T(1,128)S(1)}, u32[]{:S(2)}, u32[]{:S(2)}) async-start(f32[32,1,1024]{2,1,0:T(1,128)} %all_to_all.46), calls=%async_computation.4 | async-start | bytes 262144 | tf_op jit(solution)/shard_map/all_to_all | solution.py:24
  369.6 7.6 %all-to-all-start.5 = ((f32[32,1,1024]{2,1,0:T(1,128)}), f32[32,1,1024]{2,1,0:T(1,128)S(1)}, u32[]{:S(2)}, u32[]{:S(2)}) async-start(f32[32,1,1024]{2,1,0:T(1,128)} %broadcast_in_dim.128), calls=%async_computation.5 | async-start | bytes 262144 | tf_op jit(solution)/shard_map/all_to_all | solution.py:20
  379.5 6.2 %dynamic_update_slice.12 = f32[2,128,2048]{2,0,1:T(2,128)S(1)} dynamic-update-slice(f32[2,128,2048]{2,0,1:T(2,128)S(1)} %broadcast_in_dim.110, f32[2,32,512]{2,0,1:T(2,128)S(1)} %slice_bitcast_fusion.3, s32[]{:T(128)} %constant.123.clone.1, s32[]{:T(128)S(6)} %select_n.297, s32[]{:T(128)S(6)} %select_n.298) | dynamic-update-slice | bytes 262148 | tf_op jit(solution)/shard_map/dynamic_update_slice | solution.py:153
  386.8 6.2 %dynamic_update_slice.13 = f32[2,128,2048]{2,0,1:T(2,128)S(1)} dynamic-update-slice(f32[2,128,2048]{2,0,1:T(2,128)S(1)} %dynamic_update_slice.12, f32[2,32,512]{2,0,1:T(2,128)S(1)} %fusion.47, s32[]{:T(128)} %constant.123.clone.1, s32[]{:T(128)S(6)} %select_n.299, s32[]{:T(128)S(6)} %select_n.298) | dynamic-update-slice | bytes 262148 | tf_op jit(solution)/shard_map/dynamic_update_slice | solution.py:153
  394.1 6.2 %dynamic_update_slice.14 = f32[2,128,2048]{2,0,1:T(2,128)S(1)} dynamic-update-slice(f32[2,128,2048]{2,0,1:T(2,128)S(1)} %dynamic_update_slice.13, f32[2,32,512]{2,0,1:T(2,128)S(1)} %fusion.46, s32[]{:T(128)} %constant.123.clone.1, s32[]{:T(128)S(6)} %select_n.300, s32[]{:T(128)S(6)} %select_n.301) | dynamic-update-slice | bytes 262148 | tf_op jit(solution)/shard_map/dynamic_update_slice | solution.py:153
  401.5 6.2 %dynamic_update_slice.15 = f32[2,128,2048]{2,0,1:T(2,128)S(1)} dynamic-update-slice(f32[2,128,2048]{2,0,1:T(2,128)S(1)} %dynamic_update_slice.14, f32[2,32,512]{2,0,1:T(2,128)S(1)} %fusion.45, s32[]{:T(128)} %constant.123.clone.1, s32[]{:T(128)S(6)} %select_n.302, s32[]{:T(128)S(6)} %select_n.301) | dynamic-update-slice | bytes 262148 | tf_op jit(solution)/shard_map/dynamic_update_slice | solution.py:153
  413.2 8.1 %all-to-all-start.3 = ((f32[32,2,128,64]{2,3,1,0:T(8,128)}), f32[32,2,128,64]{2,3,1,0:T(8,128)S(1)}, u32[]{:S(2)}, u32[]{:S(2)}) async-start(f32[32,2,128,64]{2,3,1,0:T(8,128)} %copy.74), calls=%async_computation.3 | async-start | bytes 4194304 | tf_op jit(solution)/shard_map/all_to_all | solution.py:24
  422.3 49.1 %all-to-all-done.3 = f32[32,2,128,64]{2,3,1,0:T(8,128)S(1)} async-done(((f32[32,2,128,64]{2,3,1,0:T(8,128)}), f32[32,2,128,64]{2,3,1,0:T(8,128)S(1)}, u32[]{:S(2)}, u32[]{:S(2)}) %all-to-all-start.3) | async-done | bytes 2097184 | tf_op jit(solution)/shard_map/all_to_all | solution.py:24
  (156 shorter events, 184.5 us)
Async XLA Ops:
  0.6 78.0 %copy-start = (bf16[2,512,512]{2,1,0:T(8,128)(2,1)S(1)}, bf16[2,512,512]{2,1,0:T(8,128)(2,1)}, u32[]{:S(2)}) copy-start(bf16[2,512,512]{2,1,0:T(8,128)(2,1)} %param.6) | copy-start | bytes 3145732
  2.1 14.6 %copy-start.3 = (s32[64,2]{0,1:T(2,128)S(1)}, s32[64,2]{0,1:T(2,128)}, u32[]{:S(2)}) copy-start(s32[64,2]{0,1:T(2,128)} %param.7) | copy-start | bytes 1540
  2.1 14.7 %copy-start.6 = (s32[2]{0:T(128)S(1)}, s32[2]{0:T(128)}, u32[]{:S(2)}) copy-start(s32[2]{0:T(128)} %param.8) | copy-start | bytes 28
  2.1 15.5 %copy-start.4 = (s32[3]{0:T(128)S(1)}, s32[3]{0:T(128)}, u32[]{:S(2)}) copy-start(s32[3]{0:T(128)} %constant.136.clone.1) | copy-start | bytes 40
  4.4 40.6 %all-to-all-start = ((bf16[32,2,8192]{2,1,0:T(2,128)(2,1)}), bf16[32,2,8192]{2,1,0:T(2,128)(2,1)}, u32[]{:S(2)}, u32[]{:S(2)}) async-start(bf16[32,2,8192]{2,1,0:T(2,128)(2,1)} %reshape.391), calls=%async_computation | async-start | bytes 2097152 | tf_op jit(solution)/shard_map/all_to_all | solution.py:20
  63.9 12.3 %collective-permute-start = (bf16[2,2,2,32,512]{4,2,0,3,1:T(2,128)(2,1)S(1)}, bf16[2,2,2,32,512]{4,2,0,3,1:T(2,128)(2,1)S(1)}, u32[]{:S(2)}, u32[]{:S(2)}) collective-permute-start(bf16[2,2,2,32,512]{4,2,0,3,1:T(2,128)(2,1)S(1)} %pad_maximum_fusion.1), channel_id=1, source_target_pairs={{480,0},{0,32},{32,64},{64,96},{96,128},{128,160},{160,192},{192,2... | collective-permute-start | bytes 786440 | tf_op jit(solution)/shard_map/ppermute | solution.py:14
  76.7 18.1 %collective-permute-start.1 = (bf16[2,2,2,32,512]{4,2,0,3,1:T(2,128)(2,1)S(1)}, bf16[2,2,2,32,512]{4,2,0,3,1:T(2,128)(2,1)S(1)}, u32[]{:S(2)}, u32[]{:S(2)}) collective-permute-start(bf16[2,2,2,32,512]{4,2,0,3,1:T(2,128)(2,1)S(1)} %broadcast_select_fusion.4), channel_id=1, source_target_pairs={{448,0},{480,32},{0,64},{32,96},{64,128},{96,160},{128,192},{160,2... | collective-permute-start | bytes 786440 | tf_op jit(solution)/shard_map/ppermute | solution.py:14
  95.3 17.8 %collective-permute-start.2 = (bf16[2,2,2,32,512]{4,2,0,3,1:T(2,128)(2,1)S(1)}, bf16[2,2,2,32,512]{4,2,0,3,1:T(2,128)(2,1)S(1)}, u32[]{:S(2)}, u32[]{:S(2)}) collective-permute-start(bf16[2,2,2,32,512]{4,2,0,3,1:T(2,128)(2,1)S(1)} %broadcast_select_fusion.5), channel_id=1, source_target_pairs={{384,0},{416,32},{448,64},{480,96},{0,128},{32,160},{64,192},{96,2... | collective-permute-start | bytes 786440 | tf_op jit(solution)/shard_map/ppermute | solution.py:14
  113.5 9.9 %collective-permute-start.3 = (bf16[2,2,2,32,512]{4,2,0,3,1:T(2,128)(2,1)S(1)}, bf16[2,2,2,32,512]{4,2,0,3,1:T(2,128)(2,1)S(1)}, u32[]{:S(2)}, u32[]{:S(2)}) collective-permute-start(bf16[2,2,2,32,512]{4,2,0,3,1:T(2,128)(2,1)S(1)} %broadcast_select_fusion.6), channel_id=1, source_target_pairs={{256,0},{288,32},{320,64},{352,96},{384,128},{416,160},{448,192},{... | collective-permute-start | bytes 786440 | tf_op jit(solution)/shard_map/ppermute | solution.py:14
  124.0 5.7 %collective-permute-start.4 = (bf16[2,2,32,512]{3,1,0,2:T(2,128)(2,1)S(1)}, bf16[2,2,32,512]{3,1,0,2:T(2,128)(2,1)S(1)}, u32[]{:S(2)}, u32[]{:S(2)}) collective-permute-start(bf16[2,2,32,512]{3,1,0,2:T(2,128)(2,1)S(1)} %broadcast_select_fusion.8), channel_id=1, source_target_pairs={{32,0},{64,32},{96,64},{128,96},{160,128},{192,160},{224,192},{256... | collective-permute-start | bytes 393224 | tf_op jit(solution)/shard_map/ppermute | solution.py:14
  186.6 5.2 %copy-start.5 = (f32[2,32,512]{2,1,0:T(8,128)S(1)}, f32[2,32,512]{2,1,0:T(8,128)}, u32[]{:S(2)}) copy-start(f32[2,32,512]{2,1,0:T(8,128)} %param.9) | copy-start | bytes 393220
  213.7 13.3 %all-to-all-start.2 = ((f32[16,1,4096]{2,1,0:T(1,128)}), f32[16,1,4096]{2,1,0:T(1,128)S(1)}, u32[]{:S(2)}, u32[]{:S(2)}) async-start(f32[16,1,4096]{2,1,0:T(1,128)} %reshape.395), calls=%async_computation.2 | async-start | bytes 524288 | tf_op jit(solution)/shard_map/all_to_all | solution.py:137
  244.6 5.4 %copy-start.2 = (s32[4]{0:T(128)S(1)}, s32[4]{0:T(128)}, u32[]{:S(2)}) copy-start(s32[4]{0:T(128)} %constant.501) | copy-start | bytes 52
  264.8 10.7 %collective-permute-start.5 = (f32[2,2,32,512]{3,1,0,2:T(2,128)S(1)}, f32[2,2,32,512]{3,1,0,2:T(2,128)S(1)}, u32[]{:S(2)}, u32[]{:S(2)}) collective-permute-start(f32[2,2,32,512]{3,1,0,2:T(2,128)S(1)} %slice.79), channel_id=1, source_target_pairs={{480,0},{0,32},{32,64},{64,96},{96,128},{128,160},{160,192},{192,2... | collective-permute-start | bytes 786440 | tf_op jit(solution)/shard_map/ppermute | solution.py:14
  276.0 13.5 %collective-permute-start.6 = (f32[2,2,2,32,512]{4,2,0,3,1:T(2,128)S(1)}, f32[2,2,2,32,512]{4,2,0,3,1:T(2,128)S(1)}, u32[]{:S(2)}, u32[]{:S(2)}) collective-permute-start(f32[2,2,2,32,512]{4,2,0,3,1:T(2,128)S(1)} %pad_maximum_fusion), channel_id=1, source_target_pairs={{480,0},{0,32},{32,64},{64,96},{96,128},{128,160},{160,192},{192,2... | collective-permute-start | bytes 1572872 | tf_op jit(solution)/shard_map/ppermute | solution.py:14
  289.9 18.6 %collective-permute-start.7 = (f32[2,2,2,32,512]{4,2,0,3,1:T(2,128)S(1)}, f32[2,2,2,32,512]{4,2,0,3,1:T(2,128)S(1)}, u32[]{:S(2)}, u32[]{:S(2)}) collective-permute-start(f32[2,2,2,32,512]{4,2,0,3,1:T(2,128)S(1)} %broadcast_select_fusion), channel_id=1, source_target_pairs={{448,0},{480,32},{0,64},{32,96},{64,128},{96,160},{128,192},{160,2... | collective-permute-start | bytes 1572872 | tf_op jit(solution)/shard_map/ppermute | solution.py:14
  308.9 22.4 %collective-permute-start.8 = (f32[2,2,2,32,512]{4,2,0,3,1:T(2,128)S(1)}, f32[2,2,2,32,512]{4,2,0,3,1:T(2,128)S(1)}, u32[]{:S(2)}, u32[]{:S(2)}) collective-permute-start(f32[2,2,2,32,512]{4,2,0,3,1:T(2,128)S(1)} %broadcast_select_fusion.1), channel_id=1, source_target_pairs={{384,0},{416,32},{448,64},{480,96},{0,128},{32,160},{64,192},{96,2... | collective-permute-start | bytes 1572872 | tf_op jit(solution)/shard_map/ppermute | solution.py:14
  331.7 45.6 %collective-permute-start.9 = (f32[2,2,2,32,512]{4,2,0,3,1:T(2,128)S(1)}, f32[2,2,2,32,512]{4,2,0,3,1:T(2,128)S(1)}, u32[]{:S(2)}, u32[]{:S(2)}) collective-permute-start(f32[2,2,2,32,512]{4,2,0,3,1:T(2,128)S(1)} %broadcast_select_fusion.2), channel_id=1, source_target_pairs={{256,0},{288,32},{320,64},{352,96},{384,128},{416,160},{448,192},{... | collective-permute-start | bytes 1572872 | tf_op jit(solution)/shard_map/ppermute | solution.py:14
  342.2 26.6 %all-to-all-start.4 = ((f32[32,1,1024]{2,1,0:T(1,128)}), f32[32,1,1024]{2,1,0:T(1,128)S(1)}, u32[]{:S(2)}, u32[]{:S(2)}) async-start(f32[32,1,1024]{2,1,0:T(1,128)} %all_to_all.46), calls=%async_computation.4 | async-start | bytes 262144 | tf_op jit(solution)/shard_map/all_to_all | solution.py:24
  369.6 43.6 %all-to-all-start.5 = ((f32[32,1,1024]{2,1,0:T(1,128)}), f32[32,1,1024]{2,1,0:T(1,128)S(1)}, u32[]{:S(2)}, u32[]{:S(2)}) async-start(f32[32,1,1024]{2,1,0:T(1,128)} %broadcast_in_dim.128), calls=%async_computation.5 | async-start | bytes 262144 | tf_op jit(solution)/shard_map/all_to_all | solution.py:20
  377.6 0.8 copy-start.1
  413.2 58.2 %all-to-all-start.3 = ((f32[32,2,128,64]{2,3,1,0:T(8,128)}), f32[32,2,128,64]{2,3,1,0:T(8,128)S(1)}, u32[]{:S(2)}, u32[]{:S(2)}) async-start(f32[32,2,128,64]{2,3,1,0:T(8,128)} %copy.74), calls=%async_computation.3 | async-start | bytes 4194304 | tf_op jit(solution)/shard_map/all_to_all | solution.py:24

commit v2 on v1

v2 whole, which is shorter than its diff:
```python
import math

import jax
import jax.numpy as jnp
from jax import lax
from jax.sharding import PartitionSpec as P

fresnel_scale = 4


def from_behind(block, axis, distance):
    devices = range(lax.axis_size(axis))
    route = [((i - distance) % len(devices), i) for i in devices]
    return lax.ppermute(block, axis, route)


def gather_blocks(block, axis):
    count = lax.axis_size(axis)
    spread = jnp.broadcast_to(block[None], (count,) + block.shape)
    return lax.all_to_all(spread, axis, 0, 0, tiled=True)


def sum_blocks(chunks, axis):
    return jnp.sum(lax.all_to_all(chunks, axis, 0, 0, tiled=True), 0)


def dft_table(size):
    index = jnp.arange(size, dtype=jnp.int32)
    turns = index[:, None] * index[None, :] % size
    angle = 2.0 * math.pi / size * turns.astype(jnp.float32)
    norm = 1.0 / math.sqrt(size)
    return (jnp.cos(angle) * norm, -jnp.sin(angle) * norm)


def chirp_phase(index, size):
    centred = index - size // 2
    period = 2 * fresnel_scale * size
    phase = centred * centred % period
    angle = math.pi / (fresnel_scale * size) * phase.astype(jnp.float32)
    return (jnp.cos(angle), jnp.sin(angle))


def contract(form, left_side, right_side):
    return jnp.einsum(
        form,
        left_side,
        right_side,
        precision=lax.Precision.HIGHEST,
        preferred_element_type=jnp.float32,
    )


def complex_mix(form, left_re, left_im, right_re, right_im):
    real_part = contract(form, left_re, right_re) - contract(form, left_im, right_im)
    imag_part = contract(form, left_re, right_im) + contract(form, left_im, right_re)
    return (real_part, imag_part)


def on_device(object_slice, probe_field, offsets, assignment, intensities):
    depth_count = lax.axis_size("depth")
    depth_index = lax.axis_index("depth")
    scan_count = lax.axis_size("scan")
    cycles = object_slice.shape[1]
    rows_dev = object_slice.shape[2]
    patch_side = probe_field.shape[2]
    pos_count = assignment.shape[0]
    total_pos = pos_count * scan_count
    gathered = gather_blocks(object_slice, "scan")
    band = jnp.moveaxis(gathered, 0, 3).reshape(
        object_slice.shape[:3] + (scan_count * object_slice.shape[3],)
    )
    full_width = band.shape[3]
    position = offsets[assignment]
    top_row = position[:, 0]
    left_col = position[:, 1]
    table_re, table_im = dft_table(patch_side)
    twice_re = jnp.concatenate([table_re, table_re], 0)
    twice_im = jnp.concatenate([table_im, table_im], 0)
    probe_twice = jnp.concatenate([probe_field, probe_field], 1)
    row_ids = jnp.arange(rows_dev, dtype=jnp.int32)
    col_ids = jnp.arange(patch_side, dtype=jnp.int32)
    col_cos, col_sin = chirp_phase(col_ids, patch_side)
    local_rows = depth_index * rows_dev + row_ids
    shift_of = (local_rows[None, :] - top_row[:, None]) % patch_side
    cycle_of = (top_row[:, None] + shift_of) // patch_side
    obj_list, probe_list, t_re_list, t_im_list = [], [], [], []
    for slot in range(pos_count):
        chosen = band[:, 0]
        for cyc in range(1, cycles):
            chosen = jnp.where((cycle_of[slot] == cyc)[None, :, None], band[:, cyc], chosen)
        obj_list.append(lax.dynamic_slice_in_dim(chosen, left_col[slot], patch_side, 2))
        first_row = (depth_index * rows_dev - top_row[slot]) % patch_side
        probe_list.append(lax.dynamic_slice_in_dim(probe_twice, first_row, rows_dev, 1))
        table_start = (patch_side - top_row[slot] % patch_side) % patch_side
        t_re_list.append(lax.dynamic_slice_in_dim(twice_re, table_start, patch_side, 0))
        t_im_list.append(lax.dynamic_slice_in_dim(twice_im, table_start, patch_side, 0))
    patch = jnp.stack(obj_list)
    probe_rows = jnp.stack(probe_list)
    shift_re = jnp.stack(t_re_list)
    shift_im = jnp.stack(t_im_list)
    row_cos, row_sin = chirp_phase(shift_of, patch_side)
    chirp_re = (
        row_cos[:, :, None] * col_cos[None, None, :] - row_sin[:, :, None] * col_sin[None, None, :]
    )
    chirp_im = (
        row_sin[:, :, None] * col_cos[None, None, :] + row_cos[:, :, None] * col_sin[None, None, :]
    )
    obj_re = patch[:, 0].astype(jnp.float32)
    obj_im = patch[:, 1].astype(jnp.float32)
    probe_re = probe_rows[:, 0].astype(jnp.float32)
    probe_im = probe_rows[:, 1].astype(jnp.float32)
    wave_re = probe_re * obj_re - probe_im * obj_im
    wave_im = probe_re * obj_im + probe_im * obj_re
    psi_re = wave_re * chirp_re - wave_im * chirp_im
    psi_im = wave_re * chirp_im + wave_im * chirp_re
    half_re, half_im = complex_mix("vk,pjk->pvj", table_re, table_im, psi_re, psi_im)
    half_re, half_im = lax.all_to_all(
        jnp.stack([half_re, half_im]), "depth", split_axis=2, concat_axis=3, tiled=True
    )
    far_re, far_im = complex_mix("pvj,pju->pvu", half_re, half_im, shift_re, shift_im)
    excess = far_re * far_re + far_im * far_im - intensities
    resid_re = excess * far_re
    resid_im = excess * far_im
    mid_re, mid_im = complex_mix("pvu,pju->pvj", resid_re, resid_im, shift_re, -shift_im)
    mid_re, mid_im = lax.all_to_all(
        jnp.stack([mid_re, mid_im]), "depth", split_axis=3, concat_axis=2, tiled=True
    )
    back_re, back_im = complex_mix("vk,pvj->pjk", table_re, -table_im, mid_re, mid_im)
    grad_re = back_re * chirp_re + back_im * chirp_im
    grad_im = back_im * chirp_re - back_re * chirp_im
    contrib = jnp.stack(
        [probe_re * grad_re + probe_im * grad_im, probe_re * grad_im - probe_im * grad_re], 1
    )
    term = jnp.stack([obj_re * grad_re + obj_im * grad_im, obj_re * grad_im - obj_im * grad_re], 1)
    grad_band = jnp.zeros((2, cycles, rows_dev, full_width), jnp.float32)
    for slot in range(pos_count):
        placed = lax.dynamic_update_slice_in_dim(
            jnp.zeros((2, rows_dev, full_width), jnp.float32), contrib[slot], left_col[slot], 2
        )
        for cyc in range(cycles):
            taken = (cycle_of[slot] == cyc)[None, :, None]
            grad_band = grad_band.at[:, cyc].add(jnp.where(taken, placed, 0.0))
    in_block = top_row % patch_side % rows_dev
    block_shift = top_row % patch_side // rows_dev
    term_twice = jnp.concatenate([term, term], 2)
    rolled = jax.vmap(lambda t, b: lax.dynamic_slice_in_dim(t, b, rows_dev, 1))(term_twice, in_block)
    upper = (row_ids[None, :] >= rows_dev - in_block[:, None])[:, None, :, None]
    lower_part = jnp.where(upper, 0.0, rolled)
    upper_part = jnp.where(upper, rolled, 0.0)
    joined = lower_part + from_behind(upper_part, "depth", depth_count - 1)
    levels = depth_count.bit_length() - 1
    for level in range(levels):
        moved = from_behind(joined, "depth", depth_count - (1 << level))
        taken = (block_shift >> level & 1) == 1
        joined = jnp.where(taken[:, None, None, None], moved, joined)
    probe_sum = jnp.sum(joined, 0)
    probe_part = sum_blocks(probe_sum.reshape(scan_count, -1), "scan")
    probe_grad = gather_blocks(probe_part, "scan").reshape(probe_sum.shape)
    col_chunks = grad_band.reshape(2, cycles, rows_dev, scan_count, full_width // scan_count)
    object_grad = sum_blocks(jnp.moveaxis(col_chunks, 3, 0), "scan")
    return (object_grad, probe_grad * total_pos ** (-0.5))


def solution(mesh):
    return jax.shard_map(
        on_device,
        mesh=mesh,
        in_specs=(P(None, None, "depth", "scan"), P(), P(), P("scan"), P("scan", "depth", None)),
        out_specs=(P(None, None, "depth", "scan"), P(None, "depth", None)),
        check_vma=False,
    )
```

time: 480 us -> 351 us (0.73)
  the two profiles are of different devices: /device:TPU:7 before, /device:TPU:59 now
where the time goes in v2:
time: 351 us; the launch traced here: 345 us
  waiting for transfers between devices  132 us (38%)
  starting transfers between devices  62 us (18%)
  local copies, waits for them, and re-layouts  54.5 us (16%)
  matrix products  53.9 us (15%)
  other arithmetic  32.3 us (9%)
  between operations  10.5 us (3%)
    all_to_all x2, waiting for transfers between devices, sum_blocks(): return jnp.sum(lax.all_to_all(chunks, axis, 0, 0, tiled=True), 0)  57.1 us
    dot_general x16, matrix products, contract(): jnp.einsum(form, left_side, right_side, precision=lax.Precision.HIGHEST,...  53.9 us
    ppermute x5, waiting for transfers between devices, from_behind(): return lax.ppermute(block, axis, route)  51 us
    unnamed x86, local copies, waits for them, and re-layouts  21.4 us
    all_to_all x2, starting transfers between devices, gather_blocks(): return lax.all_to_all(spread, axis, 0, 0, tiled=True)  17.7 us
    all_to_all x2, starting transfers between devices, sum_blocks(): return jnp.sum(lax.all_to_all(chunks, axis, 0, 0, tiled=True), 0)  16.8 us
    all_to_all x2, waiting for transfers between devices, gather_blocks(): return lax.all_to_all(spread, axis, 0, 0, tiled=True)  16.4 us
    ppermute x5, starting transfers between devices, from_behind(): return lax.ppermute(block, axis, route)  9.84 us
  transfers between devices with their start and end apart: 11, of which 9 were waited for; matrix products, arithmetic and copies ran while one was open for 11% of the time, Pallas kernels for 0%

profile of v2, /device:TPU:59, one launch (start us, length us, event | category | flops | bytes accessed | tf_op | source)
XLA Modules:
  0.0 345.1 jit_solution(874172798190638131)
XLA Ops:
  4.3 12.3 %all-to-all-start = ((bf16[32,2,8192]{2,1,0:T(2,128)(2,1)}), bf16[32,2,8192]{2,1,0:T(2,128)(2,1)S(1)}, u32[]{:S(2)}, u32[]{:S(2)}) async-start(bf16[32,2,8192]{2,1,0:T(2,128)(2,1)} %reshape.617), calls=%async_computation | async-start | bytes 2097152 | tf_op jit(solution)/shard_map/all_to_all | solution.py:20
  28.5 16.4 %all-to-all-done = bf16[32,2,8192]{2,1,0:T(2,128)(2,1)S(1)} async-done(((bf16[32,2,8192]{2,1,0:T(2,128)(2,1)}), bf16[32,2,8192]{2,1,0:T(2,128)(2,1)S(1)}, u32[]{:S(2)}, u32[]{:S(2)}) %all-to-all-start) | async-done | bytes 1048608 | tf_op jit(solution)/shard_map/all_to_all | solution.py:20
  50.4 5.0 %fusion.39 = f32[2,32,512]{2,1,0:T(8,128)S(1)} fusion(f32[512]{0:T(512)S(1)} %get-tuple-element.153, f32[2,32]{1,0:T(2,128)S(1)} %get-tuple-element.145, f32[512]{0:T(512)S(1)} %get-tuple-element.154, f32[2,32]{1,0:T(2,128)S(1)} %get-tuple-element.144, bf16[2,32,512]{2,1,0:T(8,128)(2,1)S(1)} %get-tuple-element.133, ...), kind=kOutput, calls=%fused_computation.52 | convolution fusion | flops 205881344 | bytes 397824 | tf_op jit(solution)/shard_map/vk,pjk->pvj/dot_general | solution.py:44
  55.4 5.0 %fusion.37 = f32[2,32,512]{2,1,0:T(8,128)S(1)} fusion(f32[512]{0:T(512)S(1)} %get-tuple-element.153, f32[2,32]{1,0:T(2,128)S(1)} %get-tuple-element.145, f32[512]{0:T(512)S(1)} %get-tuple-element.154, f32[2,32]{1,0:T(2,128)S(1)} %get-tuple-element.144, bf16[2,32,512]{2,1,0:T(8,128)(2,1)S(1)} %get-tuple-element.133, ...), kind=kOutput, calls=%fused_computation.50 | convolution fusion | flops 205881344 | bytes 397824 | tf_op jit(solution)/shard_map/vk,pjk->pvj/dot_general | solution.py:44
  60.4 5.2 %fusion.5 = f32[1,2,512,32]{2,3,1,0:T(8,128)S(1)} fusion(f32[2,32,512]{2,1,0:T(8,128)S(1)} %fusion.39, f32[512]{0:T(512)S(1)} %get-tuple-element.153, f32[2,32]{1,0:T(2,128)S(1)} %get-tuple-element.145, f32[512]{0:T(512)S(1)} %get-tuple-element.154, f32[2,32]{1,0:T(2,128)S(1)} %get-tuple-element.144, bf16[2,32,512]{2,1,0:T(8,128)(2,1)S(1)} %get-tuple-element.133, ...), kind=kOutput, calls=%fused_computation.24 | convolution fusion | flops 206176256 | bytes 528896 | tf_op jit(solution)/shard_map/vk,pjk->pvj/dot_general | solution.py:44
  65.7 5.0 %fusion.4 = f32[1,2,512,32]{2,3,1,0:T(8,128)S(1)} fusion(f32[2,32,512]{2,1,0:T(8,128)S(1)} %fusion.37, f32[512]{0:T(512)S(1)} %get-tuple-element.153, f32[2,32]{1,0:T(2,128)S(1)} %get-tuple-element.145, f32[512]{0:T(512)S(1)} %get-tuple-element.154, f32[2,32]{1,0:T(2,128)S(1)} %get-tuple-element.144, bf16[2,32,512]{2,1,0:T(8,128)(2,1)S(1)} %get-tuple-element.133, ...), kind=kOutput, calls=%fused_computation.22 | convolution fusion | flops 206176256 | bytes 528896 | tf_op jit(solution)/shard_map/vk,pjk->pvj/dot_general | solution.py:44
  73.2 8.3 %all-to-all-start.1 = ((f32[16,1,4096]{2,1,0:T(1,128)}), f32[16,1,4096]{2,1,0:T(1,128)S(1)}, u32[]{:S(2)}, u32[]{:S(2)}) async-start(f32[16,1,4096]{2,1,0:T(1,128)} %reshape.619), calls=%async_computation.1 | async-start | bytes 524288 | tf_op jit(solution)/shard_map/all_to_all | solution.py:117
  119.3 9.4 %all-to-all-start.2 = ((f32[16,1,4096]{2,1,0:T(1,128)}), f32[16,1,4096]{2,1,0:T(1,128)S(1)}, u32[]{:S(2)}, u32[]{:S(2)}) async-start(f32[16,1,4096]{2,1,0:T(1,128)} %reshape.621), calls=%async_computation.2 | async-start | bytes 524288 | tf_op jit(solution)/shard_map/all_to_all | solution.py:125
  130.0 7.4 %all-to-all-done.2 = f32[16,1,4096]{2,1,0:T(1,128)S(1)} async-done(((f32[16,1,4096]{2,1,0:T(1,128)}), f32[16,1,4096]{2,1,0:T(1,128)S(1)}, u32[]{:S(2)}, u32[]{:S(2)}) %all-to-all-start.2) | async-done | bytes 262176 | tf_op jit(solution)/shard_map/all_to_all | solution.py:125
  155.1 5.1 %fusion.62 = (f32[2,1,32,512]{3,2,0,1:T(8,128)S(1)}, f32[2,32,512]{2,1,0:T(8,128)S(1)}, f32[2,32,512]{2,1,0:T(8,128)S(1)}) fusion(bf16[2,32,512]{2,1,0:T(8,128)(2,1)S(1)} %copy-done.6, bf16[2,32,512]{2,1,0:T(8,128)(2,1)S(1)} %get-tuple-element.132, f32[2,32,512]{2,1,0:T(8,128)S(1)} %convolution_add_fusion, f32[512]{0:T(512)S(1)} %copy-done.21, ...), kind=kOutput, calls=%fused_computation.114 | convolution fusion | flops 206372864 | bytes 922112 | tf_op jit(solution)/shard_map/vk,pvj->pjk/dot_general | solution.py:44
  168.6 5.0 %collective-permute-done = f32[2,2,32,512]{3,1,2,0:T(2,128)} collective-permute-done((f32[2,2,32,512]{3,1,2,0:T(2,128)}, f32[2,2,32,512]{3,1,2,0:T(2,128)}, u32[]{:S(2)}, u32[]{:S(2)}) %collective-permute-start) | collective-permute-done | bytes 262176 | tf_op jit(solution)/shard_map/ppermute | solution.py:14
  176.9 8.6 %collective-permute-done.1 = f32[2,2,32,512]{3,1,2,0:T(2,128)S(1)} collective-permute-done((f32[2,2,32,512]{3,1,2,0:T(2,128)S(1)}, f32[2,2,32,512]{3,1,2,0:T(2,128)S(1)}, u32[]{:S(2)}, u32[]{:S(2)}) %collective-permute-start.1) | collective-permute-done | bytes 262176 | tf_op jit(solution)/shard_map/ppermute | solution.py:14
  187.9 14.2 %collective-permute-done.2 = f32[2,2,32,512]{3,1,2,0:T(2,128)S(1)} collective-permute-done((f32[2,2,32,512]{3,1,2,0:T(2,128)S(1)}, f32[2,2,32,512]{3,1,2,0:T(2,128)S(1)}, u32[]{:S(2)}, u32[]{:S(2)}) %collective-permute-start.2) | collective-permute-done | bytes 262176 | tf_op jit(solution)/shard_map/ppermute | solution.py:14
  204.4 15.8 %collective-permute-done.3 = f32[2,2,32,512]{3,1,2,0:T(2,128)S(1)} collective-permute-done((f32[2,2,32,512]{3,1,2,0:T(2,128)S(1)}, f32[2,2,32,512]{3,1,2,0:T(2,128)S(1)}, u32[]{:S(2)}, u32[]{:S(2)}) %collective-permute-start.3) | collective-permute-done | bytes 262176 | tf_op jit(solution)/shard_map/ppermute | solution.py:14
  222.6 7.3 %collective-permute-done.4 = f32[2,2,32,512]{3,1,2,0:T(2,128)S(1)} collective-permute-done((f32[2,2,32,512]{3,1,2,0:T(2,128)S(1)}, f32[2,2,32,512]{3,1,2,0:T(2,128)S(1)}, u32[]{:S(2)}, u32[]{:S(2)}) %collective-permute-start.4) | collective-permute-done | bytes 262176 | tf_op jit(solution)/shard_map/ppermute | solution.py:14
  231.0 8.0 %all-to-all-start.4 = ((f32[32,1,1024]{2,1,0:T(1,128)}), f32[32,1,1024]{2,1,0:T(1,128)S(1)}, u32[]{:S(2)}, u32[]{:S(2)}) async-start(f32[32,1,1024]{2,1,0:T(1,128)} %all_to_all.49), calls=%async_computation.4 | async-start | bytes 262144 | tf_op jit(solution)/shard_map/all_to_all | solution.py:24
  239.2 8.2 %all-to-all-done.4 = f32[32,1,1024]{2,1,0:T(1,128)S(1)} async-done(((f32[32,1,1024]{2,1,0:T(1,128)}), f32[32,1,1024]{2,1,0:T(1,128)S(1)}, u32[]{:S(2)}, u32[]{:S(2)}) %all-to-all-start.4) | async-done | bytes 131104 | tf_op jit(solution)/shard_map/all_to_all | solution.py:24
  248.3 5.4 %all-to-all-start.5 = ((f32[32,1,1024]{2,1,0:T(1,128)}), f32[32,1,1024]{2,1,0:T(1,128)S(1)}, u32[]{:S(2)}, u32[]{:S(2)}) async-start(f32[32,1,1024]{2,1,0:T(1,128)} %broadcast_in_dim.181), calls=%async_computation.5 | async-start | bytes 262144 | tf_op jit(solution)/shard_map/all_to_all | solution.py:20
  255.4 4.9 %reshape.590 = f32[2,4,32,32,64]{4,3,2,1,0:T(8,128)} reshape(f32[2,4,32,2048]{3,2,1,0:T(8,128)} %copy.40) | data formatting | bytes 4194304 | tf_op jit(solution)/shard_map/reshape | solution.py:159
  260.2 6.7 %copy.58 = f32[32,2,4,32,64]{4,3,1,2,0:T(8,128)} copy(f32[32,2,4,32,64]{4,0,3,2,1:T(8,128)} %bitcast.171) | data formatting | bytes 4194304 | tf_op jit(solution)/shard_map/transpose | solution.py:160
  266.9 5.5 %reshape.623 = f32[32,1,16384]{2,1,0:T(1,128)} reshape(f32[32,4,2,32,64]{4,3,2,1,0:T(8,128)} %bitcast.172) | data formatting | bytes 4194304
  272.4 8.8 %all-to-all-start.3 = ((f32[32,1,16384]{2,1,0:T(1,128)}), f32[32,1,16384]{2,1,0:T(1,128)}, u32[]{:S(2)}, u32[]{:S(2)}) async-start(f32[32,1,16384]{2,1,0:T(1,128)} %reshape.623), calls=%async_computation.3 | async-start | bytes 4194304 | tf_op jit(solution)/shard_map/all_to_all | solution.py:24
  282.2 48.9 %all-to-all-done.3 = f32[32,1,16384]{2,1,0:T(1,128)} async-done(((f32[32,1,16384]{2,1,0:T(1,128)}), f32[32,1,16384]{2,1,0:T(1,128)}, u32[]{:S(2)}, u32[]{:S(2)}) %all-to-all-start.3) | async-done | bytes 2097184 | tf_op jit(solution)/shard_map/all_to_all | solution.py:24
  331.1 7.4 %reduce.27 = f32[32,16384]{1,0:T(8,128)S(1)} reduce(f32[32,1,16384]{2,1,0:T(1,128)} %all-to-all-done.3, f32[]{:T(128)} %broadcast.841), dimensions={1}, to_apply=%all_to_all.45.reduce_sub_computation | reduce | bytes 4194308 | tf_op jit(solution)/shard_map/all_to_all | solution.py:24
  (175 shorter events, 100.8 us)
Async XLA Ops:
  4.3 23.2 %copy-start.2 = (bf16[2,512,512]{2,1,0:T(8,128)(2,1)S(1)}, bf16[2,512,512]{2,1,0:T(8,128)(2,1)}, u32[]{:S(2)}) copy-start(bf16[2,512,512]{2,1,0:T(8,128)(2,1)} %param.22) | copy-start | bytes 3145732
  4.3 40.6 %all-to-all-start = ((bf16[32,2,8192]{2,1,0:T(2,128)(2,1)}), bf16[32,2,8192]{2,1,0:T(2,128)(2,1)S(1)}, u32[]{:S(2)}, u32[]{:S(2)}) async-start(bf16[32,2,8192]{2,1,0:T(2,128)(2,1)} %reshape.617), calls=%async_computation | async-start | bytes 2097152 | tf_op jit(solution)/shard_map/all_to_all | solution.py:20
  26.8 38.9 %copy-start.20 = (f32[512]{0:T(512)}, f32[512]{0:T(512)S(1)}, u32[]{:S(2)}) copy-start(f32[512]{0:T(512)S(1)} %get-tuple-element.153) | copy-start | bytes 6148
  26.8 38.9 %copy-start.22 = (f32[512]{0:T(512)}, f32[512]{0:T(512)S(1)}, u32[]{:S(2)}) copy-start(f32[512]{0:T(512)S(1)} %get-tuple-element.154) | copy-start | bytes 6148
  28.0 37.7 %copy-start.30 = (f32[2,32]{1,0:T(2,128)}, f32[2,32]{1,0:T(2,128)S(1)}, u32[]{:S(2)}) copy-start(f32[2,32]{1,0:T(2,128)S(1)} %get-tuple-element.144) | copy-start | bytes 772
  28.0 37.7 %copy-start.32 = (f32[2,32]{1,0:T(2,128)}, f32[2,32]{1,0:T(2,128)S(1)}, u32[]{:S(2)}) copy-start(f32[2,32]{1,0:T(2,128)S(1)} %get-tuple-element.145) | copy-start | bytes 772
  28.5 21.4 %copy-start.11 = (pred[32]{0:T(512)(128)(4,1)}, pred[32]{0:T(512)(128)(4,1)S(1)}, u32[]{:S(2)}) copy-start(pred[32]{0:T(512)(128)(4,1)S(1)} %get-tuple-element.138) | copy-start | bytes 100
  28.5 21.5 %copy-start.13 = (pred[32]{0:T(512)(128)(4,1)}, pred[32]{0:T(512)(128)(4,1)S(1)}, u32[]{:S(2)}) copy-start(pred[32]{0:T(512)(128)(4,1)S(1)} %get-tuple-element.139) | copy-start | bytes 100
  73.2 18.4 %all-to-all-start.1 = ((f32[16,1,4096]{2,1,0:T(1,128)}), f32[16,1,4096]{2,1,0:T(1,128)S(1)}, u32[]{:S(2)}, u32[]{:S(2)}) async-start(f32[16,1,4096]{2,1,0:T(1,128)} %reshape.619), calls=%async_computation.1 | async-start | bytes 524288 | tf_op jit(solution)/shard_map/all_to_all | solution.py:117
  119.3 18.0 %all-to-all-start.2 = ((f32[16,1,4096]{2,1,0:T(1,128)}), f32[16,1,4096]{2,1,0:T(1,128)S(1)}, u32[]{:S(2)}, u32[]{:S(2)}) async-start(f32[16,1,4096]{2,1,0:T(1,128)} %reshape.621), calls=%async_computation.2 | async-start | bytes 524288 | tf_op jit(solution)/shard_map/all_to_all | solution.py:125
  128.8 32.9 %copy-start.24 = (pred[2,32]{1,0:T(4,128)(4,1)}, pred[2,32]{1,0:T(4,128)(4,1)S(1)}, u32[]{:S(2)}) copy-start(pred[2,32]{1,0:T(4,128)(4,1)S(1)} %iota_compare_fusion) | copy-start | bytes 196
  162.6 11.0 %collective-permute-start = (f32[2,2,32,512]{3,1,2,0:T(2,128)}, f32[2,2,32,512]{3,1,2,0:T(2,128)}, u32[]{:S(2)}, u32[]{:S(2)}) collective-permute-start(f32[2,2,32,512]{3,1,2,0:T(2,128)} %broadcast_select_fusion.3), channel_id=1, source_target_pairs={{32,0},{64,32},{96,64},{128,96},{160,128},{192,160},{224,192},{256... | collective-permute-start | bytes 786440 | tf_op jit(solution)/shard_map/ppermute | solution.py:14
  166.7 18.8 %copy-start.28 = (pred[2]{0:T(512)(128)(4,1)S(1)}, pred[2]{0:T(512)(128)(4,1)}, u32[]{:S(2)}) copy-start(pred[2]{0:T(512)(128)(4,1)} %get-tuple-element.152) | copy-start | bytes 10
  174.8 27.3 %copy-start.27 = (pred[2]{0:T(512)(128)(4,1)S(1)}, pred[2]{0:T(512)(128)(4,1)}, u32[]{:S(2)}) copy-start(pred[2]{0:T(512)(128)(4,1)} %get-tuple-element.151) | copy-start | bytes 10
  174.8 29.4 %copy-start.18 = (pred[32]{0:T(512)(128)(4,1)S(1)}, pred[32]{0:T(512)(128)(4,1)}, u32[]{:S(2)}) copy-start(pred[32]{0:T(512)(128)(4,1)} %get-tuple-element.136) | copy-start | bytes 100
  174.8 10.7 %collective-permute-start.1 = (f32[2,2,32,512]{3,1,2,0:T(2,128)S(1)}, f32[2,2,32,512]{3,1,2,0:T(2,128)S(1)}, u32[]{:S(2)}, u32[]{:S(2)}) collective-permute-start(f32[2,2,32,512]{3,1,2,0:T(2,128)S(1)} %select_add_fusion), channel_id=1, source_target_pairs={{32,0},{64,32},{96,64},{128,96},{160,128},{192,160},{224,192},{256... | collective-permute-start | bytes 786440 | tf_op jit(solution)/shard_map/ppermute | solution.py:14
  185.7 34.5 %copy-start.26 = (pred[2]{0:T(512)(128)(4,1)S(1)}, pred[2]{0:T(512)(128)(4,1)}, u32[]{:S(2)}) copy-start(pred[2]{0:T(512)(128)(4,1)} %get-tuple-element.150) | copy-start | bytes 10
  185.8 16.3 %collective-permute-start.2 = (f32[2,2,32,512]{3,1,2,0:T(2,128)S(1)}, f32[2,2,32,512]{3,1,2,0:T(2,128)S(1)}, u32[]{:S(2)}, u32[]{:S(2)}) collective-permute-start(f32[2,2,32,512]{3,1,2,0:T(2,128)S(1)} %broadcast_select_fusion), channel_id=1, source_target_pairs={{64,0},{96,32},{128,64},{160,96},{192,128},{224,160},{256,192},{28... | collective-permute-start | bytes 786440 | tf_op jit(solution)/shard_map/ppermute | solution.py:14
  202.3 27.6 %copy-start.35 = (pred[2]{0:T(512)(128)(4,1)S(1)}, pred[2]{0:T(512)(128)(4,1)}, u32[]{:S(2)}) copy-start(pred[2]{0:T(512)(128)(4,1)} %get-tuple-element.104) | copy-start | bytes 10
  202.3 17.9 %collective-permute-start.3 = (f32[2,2,32,512]{3,1,2,0:T(2,128)S(1)}, f32[2,2,32,512]{3,1,2,0:T(2,128)S(1)}, u32[]{:S(2)}, u32[]{:S(2)}) collective-permute-start(f32[2,2,32,512]{3,1,2,0:T(2,128)S(1)} %broadcast_select_fusion.1), channel_id=1, source_target_pairs={{128,0},{160,32},{192,64},{224,96},{256,128},{288,160},{320,192},{... | collective-permute-start | bytes 786440 | tf_op jit(solution)/shard_map/ppermute | solution.py:14
  220.4 9.5 %collective-permute-start.4 = (f32[2,2,32,512]{3,1,2,0:T(2,128)S(1)}, f32[2,2,32,512]{3,1,2,0:T(2,128)S(1)}, u32[]{:S(2)}, u32[]{:S(2)}) collective-permute-start(f32[2,2,32,512]{3,1,2,0:T(2,128)S(1)} %broadcast_select_fusion.2), channel_id=1, source_target_pairs={{256,0},{288,32},{320,64},{352,96},{384,128},{416,160},{448,192},{... | collective-permute-start | bytes 786440 | tf_op jit(solution)/shard_map/ppermute | solution.py:14
  231.0 16.5 %all-to-all-start.4 = ((f32[32,1,1024]{2,1,0:T(1,128)}), f32[32,1,1024]{2,1,0:T(1,128)S(1)}, u32[]{:S(2)}, u32[]{:S(2)}) async-start(f32[32,1,1024]{2,1,0:T(1,128)} %all_to_all.49), calls=%async_computation.4 | async-start | bytes 262144 | tf_op jit(solution)/shard_map/all_to_all | solution.py:24
  248.3 24.1 %all-to-all-start.5 = ((f32[32,1,1024]{2,1,0:T(1,128)}), f32[32,1,1024]{2,1,0:T(1,128)S(1)}, u32[]{:S(2)}, u32[]{:S(2)}) async-start(f32[32,1,1024]{2,1,0:T(1,128)} %broadcast_in_dim.181), calls=%async_computation.5 | async-start | bytes 262144 | tf_op jit(solution)/shard_map/all_to_all | solution.py:20
  272.4 58.8 %all-to-all-start.3 = ((f32[32,1,16384]{2,1,0:T(1,128)}), f32[32,1,16384]{2,1,0:T(1,128)}, u32[]{:S(2)}, u32[]{:S(2)}) async-start(f32[32,1,16384]{2,1,0:T(1,128)} %reshape.623), calls=%async_computation.3 | async-start | bytes 4194304 | tf_op jit(solution)/shard_map/all_to_all | solution.py:24
  (24 other events, 167.5 us)

commit v3 on v2

--- a/solution.py
+++ b/solution.py
@@ -65,11 +65,10 @@
     patch_side = probe_field.shape[2]
     pos_count = assignment.shape[0]
     total_pos = pos_count * scan_count
-    gathered = gather_blocks(object_slice, "scan")
-    band = jnp.moveaxis(gathered, 0, 3).reshape(
-        object_slice.shape[:3] + (scan_count * object_slice.shape[3],)
-    )
-    full_width = band.shape[3]
+    width = object_slice.shape[3]
+    full_width = scan_count * width
+    all_slots = gather_blocks(assignment, "scan").reshape(total_pos)
+    every_top = offsets[all_slots, 0]
     position = offsets[assignment]
     top_row = position[:, 0]
     left_col = position[:, 1]
@@ -81,14 +80,19 @@
     col_ids = jnp.arange(patch_side, dtype=jnp.int32)
     col_cos, col_sin = chirp_phase(col_ids, patch_side)
     local_rows = depth_index * rows_dev + row_ids
+    every_cycle = (every_top[:, None] + (local_rows[None, :] - every_top[:, None]) % patch_side) // patch_side
+    picked = jnp.broadcast_to(object_slice[:, 0][None], (total_pos,) + object_slice[:, 0].shape)
+    for cyc in range(1, cycles):
+        picked = jnp.where((every_cycle == cyc)[:, None, :, None], object_slice[:, cyc][None], picked)
+    received = lax.all_to_all(
+        picked.reshape((scan_count, pos_count) + picked.shape[1:]), "scan", 0, 0, tiled=True
+    )
+    band = jnp.moveaxis(received, 0, 3).reshape(pos_count, 2, rows_dev, full_width)
     shift_of = (local_rows[None, :] - top_row[:, None]) % patch_side
     cycle_of = (top_row[:, None] + shift_of) // patch_side
     obj_list, probe_list, t_re_list, t_im_list = [], [], [], []
     for slot in range(pos_count):
-        chosen = band[:, 0]
-        for cyc in range(1, cycles):
-            chosen = jnp.where((cycle_of[slot] == cyc)[None, :, None], band[:, cyc], chosen)
-        obj_list.append(lax.dynamic_slice_in_dim(chosen, left_col[slot], patch_side, 2))
+        obj_list.append(lax.dynamic_slice_in_dim(band[slot], left_col[slot], patch_side, 2))
         first_row = (depth_index * rows_dev - top_row[slot]) % patch_side
         probe_list.append(lax.dynamic_slice_in_dim(probe_twice, first_row, rows_dev, 1))
         table_start = (patch_side - top_row[slot] % patch_side) % patch_side
@@ -132,14 +136,22 @@
         [probe_re * grad_re + probe_im * grad_im, probe_re * grad_im - probe_im * grad_re], 1
     )
     term = jnp.stack([obj_re * grad_re + obj_im * grad_im, obj_re * grad_im - obj_im * grad_re], 1)
-    grad_band = jnp.zeros((2, cycles, rows_dev, full_width), jnp.float32)
-    for slot in range(pos_count):
-        placed = lax.dynamic_update_slice_in_dim(
-            jnp.zeros((2, rows_dev, full_width), jnp.float32), contrib[slot], left_col[slot], 2
+    placed = jax.vmap(
+        lambda tile, col: lax.dynamic_update_slice_in_dim(
+            jnp.zeros((2, rows_dev, full_width), jnp.float32), tile, col, 2
         )
-        for cyc in range(cycles):
-            taken = (cycle_of[slot] == cyc)[None, :, None]
-            grad_band = grad_band.at[:, cyc].add(jnp.where(taken, placed, 0.0))
+    )(contrib, left_col)
+    grad_chunks = jnp.moveaxis(placed.reshape(pos_count, 2, rows_dev, scan_count, width), 3, 0)
+    grad_back = lax.all_to_all(grad_chunks, "scan", 0, 0, tiled=True).reshape(
+        (total_pos, 2, rows_dev, width)
+    )
+    object_grad = jnp.stack(
+        [
+            jnp.sum(jnp.where((every_cycle == cyc)[:, None, :, None], grad_back, 0.0), 0)
+            for cyc in range(cycles)
+        ],
+        1,
+    )
     in_block = top_row % patch_side % rows_dev
     block_shift = top_row % patch_side // rows_dev
     term_twice = jnp.concatenate([term, term], 2)
@@ -156,8 +168,6 @@
     probe_sum = jnp.sum(joined, 0)
     probe_part = sum_blocks(probe_sum.reshape(scan_count, -1), "scan")
     probe_grad = gather_blocks(probe_part, "scan").reshape(probe_sum.shape)
-    col_chunks = grad_band.reshape(2, cycles, rows_dev, scan_count, full_width // scan_count)
-    object_grad = sum_blocks(jnp.moveaxis(col_chunks, 3, 0), "scan")
     return (object_grad, probe_grad * total_pos ** (-0.5))
 
 

time: 351 us -> 334 us (0.952)
  the two profiles are of different devices: /device:TPU:59 before, /device:TPU:58 now
where the time goes in v3:
time: 334 us; the launch traced here: 329 us
  waiting for transfers between devices  114 us (34%)
  starting transfers between devices  71.2 us (21%)
  matrix products  53.8 us (16%)
  local copies, waits for them, and re-layouts  43.2 us (13%)
  other arithmetic  36.1 us (11%)
  between operations  11 us (3%)
    dot_general x16, matrix products, contract(): jnp.einsum(form, left_side, right_side, precision=lax.Precision.HIGHEST,...  53.8 us
    ppermute x5, waiting for transfers between devices, from_behind(): return lax.ppermute(block, axis, route)  52 us
    all_to_all x1, waiting for transfers between devices, on_device(): lax.all_to_all(grad_chunks, 'scan', 0, 0, tiled=True)  27.7 us
    all_to_all x1, waiting for transfers between devices, on_device(): lax.all_to_all(picked.reshape((scan_count, pos_count) + picked.shape[1:])...  15.9 us
    all_to_all x2, starting transfers between devices, gather_blocks(): return lax.all_to_all(spread, axis, 0, 0, tiled=True)  15.9 us
    unnamed x65, local copies, waits for them, and re-layouts  14.4 us
    ppermute x5, starting transfers between devices, from_behind(): return lax.ppermute(block, axis, route)  12 us
    scatter x4, other arithmetic  10.6 us
  transfers between devices with their start and end apart: 12, of which 9 were waited for; matrix products, arithmetic and copies ran while one was open for 12% of the time, Pallas kernels for 0%

profile of v3, /device:TPU:58, one launch (start us, length us, event | category | flops | bytes accessed | tf_op | source)
XLA Modules:
  0.0 329.4 jit_solution(15517031434052324958)
XLA Ops:
  1.9 11.9 %all-to-all-start = ((s32[32,1,2]{2,1,0:T(1,128)}), s32[32,1,2]{2,1,0:T(1,128)S(1)}, u32[]{:S(2)}, u32[]{:S(2)}) async-start(s32[32,1,2]{2,1,0:T(1,128)} %broadcast_in_dim.169), calls=%async_computation | async-start | bytes 32768 | tf_op jit(solution)/shard_map/all_to_all | solution.py:20
  33.1 8.8 %all-to-all-start.1 = ((bf16[32,2,4096]{2,1,0:T(2,128)(2,1)}), bf16[32,2,4096]{2,1,0:T(2,128)(2,1)S(1)}, u32[]{:S(2)}, u32[]{:S(2)}) async-start(bf16[32,2,4096]{2,1,0:T(2,128)(2,1)} %reshape.562), calls=%async_computation.1 | async-start | bytes 1048576 | tf_op jit(solution)/shard_map/all_to_all | solution.py:87
  43.2 15.9 %all-to-all-done.1 = bf16[32,2,4096]{2,1,0:T(2,128)(2,1)S(1)} async-done(((bf16[32,2,4096]{2,1,0:T(2,128)(2,1)}), bf16[32,2,4096]{2,1,0:T(2,128)(2,1)S(1)}, u32[]{:S(2)}, u32[]{:S(2)}) %all-to-all-start.1) | async-done | bytes 524320 | tf_op jit(solution)/shard_map/all_to_all | solution.py:87
  61.6 5.0 %fusion.39 = f32[2,32,512]{2,1,0:T(8,128)S(1)} fusion(f32[512]{0:T(512)S(1)} %get-tuple-element.88, f32[2,32]{1,0:T(2,128)S(1)} %get-tuple-element.80, f32[512]{0:T(512)S(1)} %get-tuple-element.89, f32[2,32]{1,0:T(2,128)S(1)} %get-tuple-element.79, bf16[2,32,512]{2,1,0:T(8,128)(2,1)S(1)} %get-tuple-element.67, ...), kind=kOutput, calls=%fused_computation.60 | convolution fusion | flops 205881344 | bytes 397824 | tf_op jit(solution)/shard_map/vk,pjk->pvj/dot_general | solution.py:44
  66.6 5.2 %fusion.37 = f32[2,32,512]{2,1,0:T(8,128)S(1)} fusion(f32[512]{0:T(512)S(1)} %get-tuple-element.88, f32[2,32]{1,0:T(2,128)S(1)} %get-tuple-element.80, f32[512]{0:T(512)S(1)} %get-tuple-element.89, f32[2,32]{1,0:T(2,128)S(1)} %get-tuple-element.79, bf16[2,32,512]{2,1,0:T(8,128)(2,1)S(1)} %get-tuple-element.67, ...), kind=kOutput, calls=%fused_computation.58 | convolution fusion | flops 205881344 | bytes 397824 | tf_op jit(solution)/shard_map/vk,pjk->pvj/dot_general | solution.py:44
  71.8 5.0 %fusion.5 = f32[1,2,512,32]{2,3,1,0:T(8,128)S(1)} fusion(f32[2,32,512]{2,1,0:T(8,128)S(1)} %fusion.39, f32[512]{0:T(512)S(1)} %get-tuple-element.88, f32[2,32]{1,0:T(2,128)S(1)} %get-tuple-element.80, f32[512]{0:T(512)S(1)} %get-tuple-element.89, f32[2,32]{1,0:T(2,128)S(1)} %get-tuple-element.79, bf16[2,32,512]{2,1,0:T(8,128)(2,1)S(1)} %get-tuple-element.67, ...), kind=kOutput, calls=%fused_computation.32 | convolution fusion | flops 206176256 | bytes 528896 | tf_op jit(solution)/shard_map/vk,pjk->pvj/dot_general | solution.py:44
  76.9 5.0 %fusion.4 = f32[1,2,512,32]{2,3,1,0:T(8,128)S(1)} fusion(f32[2,32,512]{2,1,0:T(8,128)S(1)} %fusion.37, f32[512]{0:T(512)S(1)} %get-tuple-element.88, f32[2,32]{1,0:T(2,128)S(1)} %get-tuple-element.80, f32[512]{0:T(512)S(1)} %get-tuple-element.89, f32[2,32]{1,0:T(2,128)S(1)} %get-tuple-element.79, bf16[2,32,512]{2,1,0:T(8,128)(2,1)S(1)} %get-tuple-element.67, ...), kind=kOutput, calls=%fused_computation.30 | convolution fusion | flops 206176256 | bytes 528896 | tf_op jit(solution)/shard_map/vk,pjk->pvj/dot_general | solution.py:44
  84.4 8.6 %all-to-all-start.2 = ((f32[16,1,4096]{2,1,0:T(1,128)}), f32[16,1,4096]{2,1,0:T(1,128)S(1)}, u32[]{:S(2)}, u32[]{:S(2)}) async-start(f32[16,1,4096]{2,1,0:T(1,128)} %reshape.564), calls=%async_computation.2 | async-start | bytes 524288 | tf_op jit(solution)/shard_map/all_to_all | solution.py:121
  131.0 9.9 %all-to-all-start.3 = ((f32[16,1,4096]{2,1,0:T(1,128)}), f32[16,1,4096]{2,1,0:T(1,128)S(1)}, u32[]{:S(2)}, u32[]{:S(2)}) async-start(f32[16,1,4096]{2,1,0:T(1,128)} %reshape.566), calls=%async_computation.3 | async-start | bytes 524288 | tf_op jit(solution)/shard_map/all_to_all | solution.py:129
  141.1 9.4 %all-to-all-done.3 = f32[16,1,4096]{2,1,0:T(1,128)S(1)} async-done(((f32[16,1,4096]{2,1,0:T(1,128)}), f32[16,1,4096]{2,1,0:T(1,128)S(1)}, u32[]{:S(2)}, u32[]{:S(2)}) %all-to-all-start.3) | async-done | bytes 262176 | tf_op jit(solution)/shard_map/all_to_all | solution.py:129
  153.6 4.8 %fusion.33 = f32[2,32,512]{2,1,0:T(8,128)S(1)} fusion(f32[2,512,32]{1,2,0:T(8,128)S(1)} %unstack.31), kind=kOutput, calls=%fused_computation.54 | convolution fusion | flops 205258752 | bytes 262144 | tf_op jit(solution)/shard_map/vk,pvj->pjk/dot_general | solution.py:44
  158.6 4.8 %fusion.35 = f32[2,32,512]{2,1,0:T(8,128)S(1)} fusion(f32[2,512,32]{1,2,0:T(8,128)S(1)} %unstack.29), kind=kOutput, calls=%fused_computation.56 | convolution fusion | flops 205258752 | bytes 262144 | tf_op jit(solution)/shard_map/vk,pvj->pjk/dot_general | solution.py:44
  163.4 4.8 %convolution_add_fusion = f32[2,32,512]{2,1,0:T(8,128)S(1)} fusion(f32[2,32,512]{2,1,0:T(8,128)S(1)} %fusion.33, f32[2,512,32]{1,2,0:T(8,128)S(1)} %unstack.29), kind=kOutput, calls=%fused_computation.27 | convolution fusion | flops 205815808 | bytes 393216 | tf_op jit(solution)/shard_map/vk,pvj->pjk/dot_general | solution.py:44
  168.2 5.1 %fusion.56 = (f32[2,1,32,512]{3,2,0,1:T(8,128)S(1)}, f32[2,32,512]{2,1,0:T(8,128)S(1)}, f32[2,32,512]{2,1,0:T(8,128)S(1)}) fusion(bf16[2,32,512]{2,1,0:T(8,128)(2,1)S(1)} %copy-done.7, bf16[2,32,512]{2,1,0:T(8,128)(2,1)S(1)} %copy-done.5, f32[2,32,512]{2,1,0:T(8,128)S(1)} %convolution_add_fusion, f32[512]{0:T(512)S(1)} %copy-done.17, ...), kind=kOutput, calls=%fused_computation.104 | convolution fusion | flops 206372864 | bytes 922112 | tf_op jit(solution)/shard_map/vk,pvj->pjk/dot_general | solution.py:44
  177.5 9.2 %collective-permute-done = f32[2,2,32,512]{3,1,2,0:T(2,128)S(1)} collective-permute-done((f32[2,2,32,512]{3,1,2,0:T(2,128)S(1)}, f32[2,2,32,512]{3,1,2,0:T(2,128)S(1)}, u32[]{:S(2)}, u32[]{:S(2)}) %collective-permute-start) | collective-permute-done | bytes 262176 | tf_op jit(solution)/shard_map/ppermute | solution.py:14
  189.0 10.6 %collective-permute-done.1 = f32[2,2,32,512]{3,1,2,0:T(2,128)S(1)} collective-permute-done((f32[2,2,32,512]{3,1,2,0:T(2,128)S(1)}, f32[2,2,32,512]{3,1,2,0:T(2,128)S(1)}, u32[]{:S(2)}, u32[]{:S(2)}) %collective-permute-start.1) | collective-permute-done | bytes 262176 | tf_op jit(solution)/shard_map/ppermute | solution.py:14
  201.8 11.0 %collective-permute-done.2 = f32[2,2,32,512]{3,1,2,0:T(2,128)S(1)} collective-permute-done((f32[2,2,32,512]{3,1,2,0:T(2,128)S(1)}, f32[2,2,32,512]{3,1,2,0:T(2,128)S(1)}, u32[]{:S(2)}, u32[]{:S(2)}) %collective-permute-start.2) | collective-permute-done | bytes 262176 | tf_op jit(solution)/shard_map/ppermute | solution.py:14
  214.9 14.8 %collective-permute-done.3 = f32[2,2,32,512]{3,1,2,0:T(2,128)S(1)} collective-permute-done((f32[2,2,32,512]{3,1,2,0:T(2,128)S(1)}, f32[2,2,32,512]{3,1,2,0:T(2,128)S(1)}, u32[]{:S(2)}, u32[]{:S(2)}) %collective-permute-start.3) | collective-permute-done | bytes 262176 | tf_op jit(solution)/shard_map/ppermute | solution.py:14
  233.5 6.2 %collective-permute-done.4 = f32[2,2,32,512]{3,1,2,0:T(2,128)S(1)} collective-permute-done((f32[2,2,32,512]{3,1,2,0:T(2,128)S(1)}, f32[2,2,32,512]{3,1,2,0:T(2,128)S(1)}, u32[]{:S(2)}, u32[]{:S(2)}) %collective-permute-start.4) | collective-permute-done | bytes 262176 | tf_op jit(solution)/shard_map/ppermute | solution.py:14
  240.9 7.0 %all-to-all-start.5 = ((f32[32,1,1024]{2,1,0:T(1,128)}), f32[32,1,1024]{2,1,0:T(1,128)S(1)}, u32[]{:S(2)}, u32[]{:S(2)}) async-start(f32[32,1,1024]{2,1,0:T(1,128)} %all_to_all.54), calls=%async_computation.5 | async-start | bytes 262144 | tf_op jit(solution)/shard_map/all_to_all | solution.py:24
  248.1 9.0 %all-to-all-done.5 = f32[32,1,1024]{2,1,0:T(1,128)S(1)} async-done(((f32[32,1,1024]{2,1,0:T(1,128)}), f32[32,1,1024]{2,1,0:T(1,128)S(1)}, u32[]{:S(2)}, u32[]{:S(2)}) %all-to-all-start.5) | async-done | bytes 131104 | tf_op jit(solution)/shard_map/all_to_all | solution.py:24
  262.0 16.2 %while.1 = (s32[]{:T(128)}, f32[2,2,32,2048]{3,2,1,0:T(8,128)S(1)}, s32[2,4]{1,0:T(2,128)S(1)}, f32[2,2,32,512]{3,2,0,1:T(8,128)S(1)}, s32[]{:T(128)}, /*index=5*/s32[4]{0:T(128)S(1)}, s32[]{:T(128)}) while((s32[]{:T(128)}, f32[2,2,32,2048]{3,2,1,0:T(8,128)S(1)}, s32[2,4]{1,0:T(2,128)S(1)}, f32[2,2,32,512]{3,2,0,1:T(8,128)S(1)}, s32[]{:T(128)}, ...), condition=%wide.while_cond, body=%wide.while_body.sunk | while | flops 32797 | bytes 655555 | solution.py:140
  285.1 9.1 %all-to-all-start.4 = ((f32[32,1,8192]{2,1,0:T(1,128)}), f32[32,1,8192]{2,1,0:T(1,128)S(1)}, u32[]{:S(2)}, u32[]{:S(2)}) async-start(f32[32,1,8192]{2,1,0:T(1,128)} %reshape.568), calls=%async_computation.4 | async-start | bytes 2097152 | tf_op jit(solution)/shard_map/all_to_all | solution.py:145
  295.2 27.7 %all-to-all-done.4 = f32[32,1,8192]{2,1,0:T(1,128)S(1)} async-done(((f32[32,1,8192]{2,1,0:T(1,128)}), f32[32,1,8192]{2,1,0:T(1,128)S(1)}, u32[]{:S(2)}, u32[]{:S(2)}) %all-to-all-start.4) | async-done | bytes 1048608 | tf_op jit(solution)/shard_map/all_to_all | solution.py:145
  (167 shorter events, 109.4 us)
Async XLA Ops:
  1.9 24.6 %all-to-all-start = ((s32[32,1,2]{2,1,0:T(1,128)}), s32[32,1,2]{2,1,0:T(1,128)S(1)}, u32[]{:S(2)}, u32[]{:S(2)}) async-start(s32[32,1,2]{2,1,0:T(1,128)} %broadcast_in_dim.169), calls=%async_computation | async-start | bytes 32768 | tf_op jit(solution)/shard_map/all_to_all | solution.py:20
  27.8 14.2 %copy-start.1 = (bf16[2,512,512]{2,1,0:T(8,128)(2,1)S(1)}, bf16[2,512,512]{2,1,0:T(8,128)(2,1)}, u32[]{:S(2)}) copy-start(bf16[2,512,512]{2,1,0:T(8,128)(2,1)} %param.6) | copy-start | bytes 3145732
  33.1 25.9 %all-to-all-start.1 = ((bf16[32,2,4096]{2,1,0:T(2,128)(2,1)}), bf16[32,2,4096]{2,1,0:T(2,128)(2,1)S(1)}, u32[]{:S(2)}, u32[]{:S(2)}) async-start(bf16[32,2,4096]{2,1,0:T(2,128)(2,1)} %reshape.562), calls=%async_computation.1 | async-start | bytes 1048576 | tf_op jit(solution)/shard_map/all_to_all | solution.py:87
  42.0 34.8 %copy-start.16 = (f32[512]{0:T(512)}, f32[512]{0:T(512)S(1)}, u32[]{:S(2)}) copy-start(f32[512]{0:T(512)S(1)} %get-tuple-element.88) | copy-start | bytes 6148
  42.0 34.8 %copy-start.18 = (f32[512]{0:T(512)}, f32[512]{0:T(512)S(1)}, u32[]{:S(2)}) copy-start(f32[512]{0:T(512)S(1)} %get-tuple-element.89) | copy-start | bytes 6148
  43.0 17.2 %copy-start.20 = (s32[2]{0:T(128)}, s32[2]{0:T(128)S(1)}, u32[]{:S(2)}) copy-start(s32[2]{0:T(128)S(1)} %get-tuple-element.78) | copy-start | bytes 28
  43.1 33.7 %copy-start.22 = (f32[2,32]{1,0:T(2,128)}, f32[2,32]{1,0:T(2,128)S(1)}, u32[]{:S(2)}) copy-start(f32[2,32]{1,0:T(2,128)S(1)} %get-tuple-element.79) | copy-start | bytes 772
  43.1 33.7 %copy-start.24 = (f32[2,32]{1,0:T(2,128)}, f32[2,32]{1,0:T(2,128)S(1)}, u32[]{:S(2)}) copy-start(f32[2,32]{1,0:T(2,128)S(1)} %get-tuple-element.80) | copy-start | bytes 772
  61.6 15.2 %copy-start.4 = (bf16[2,32,512]{2,1,0:T(8,128)(2,1)}, bf16[2,32,512]{2,1,0:T(8,128)(2,1)S(1)}, u32[]{:S(2)}) copy-start(bf16[2,32,512]{2,1,0:T(8,128)(2,1)S(1)} %get-tuple-element.66) | copy-start | bytes 196612
  61.6 15.2 %copy-start.6 = (bf16[2,32,512]{2,1,0:T(8,128)(2,1)}, bf16[2,32,512]{2,1,0:T(8,128)(2,1)S(1)}, u32[]{:S(2)}) copy-start(bf16[2,32,512]{2,1,0:T(8,128)(2,1)S(1)} %get-tuple-element.67) | copy-start | bytes 196612
  84.4 18.7 %all-to-all-start.2 = ((f32[16,1,4096]{2,1,0:T(1,128)}), f32[16,1,4096]{2,1,0:T(1,128)S(1)}, u32[]{:S(2)}, u32[]{:S(2)}) async-start(f32[16,1,4096]{2,1,0:T(1,128)} %reshape.564), calls=%async_computation.2 | async-start | bytes 524288 | tf_op jit(solution)/shard_map/all_to_all | solution.py:121
  131.0 19.5 %all-to-all-start.3 = ((f32[16,1,4096]{2,1,0:T(1,128)}), f32[16,1,4096]{2,1,0:T(1,128)S(1)}, u32[]{:S(2)}, u32[]{:S(2)}) async-start(f32[16,1,4096]{2,1,0:T(1,128)} %reshape.566), calls=%async_computation.3 | async-start | bytes 524288 | tf_op jit(solution)/shard_map/all_to_all | solution.py:129
  173.3 15.6 %copy-start.21 = (s32[2]{0:T(128)S(1)}, s32[2]{0:T(128)}, u32[]{:S(2)}) copy-start(s32[2]{0:T(128)} %copy-done.20) | copy-start | bytes 28
  174.9 11.9 %collective-permute-start = (f32[2,2,32,512]{3,1,2,0:T(2,128)S(1)}, f32[2,2,32,512]{3,1,2,0:T(2,128)S(1)}, u32[]{:S(2)}, u32[]{:S(2)}) collective-permute-start(f32[2,2,32,512]{3,1,2,0:T(2,128)S(1)} %broadcast_select_fusion.3), channel_id=1, source_target_pairs={{32,0},{64,32},{96,64},{128,96},{160,128},{192,160},{224,192},{256... | collective-permute-start | bytes 786440 | tf_op jit(solution)/shard_map/ppermute | solution.py:14
  187.0 60.9 %copy-start.14 = (s32[2,1]{1,0:T(2,128)S(1)}, s32[2,1]{1,0:T(2,128)}, u32[]{:S(2)}) copy-start(s32[2,1]{1,0:T(2,128)} %get-tuple-element.77) | copy-start | bytes 28
  187.0 60.9 %copy-start.26 = (s32[3]{0:T(128)S(1)}, s32[3]{0:T(128)}, u32[]{:S(2)}) copy-start(s32[3]{0:T(128)} %constant.161.clone.1) | copy-start | bytes 40
  187.0 12.6 %collective-permute-start.1 = (f32[2,2,32,512]{3,1,2,0:T(2,128)S(1)}, f32[2,2,32,512]{3,1,2,0:T(2,128)S(1)}, u32[]{:S(2)}, u32[]{:S(2)}) collective-permute-start(f32[2,2,32,512]{3,1,2,0:T(2,128)S(1)} %select_add_fusion), channel_id=1, source_target_pairs={{32,0},{64,32},{96,64},{128,96},{160,128},{192,160},{224,192},{256... | collective-permute-start | bytes 786440 | tf_op jit(solution)/shard_map/ppermute | solution.py:14
  199.8 13.0 %collective-permute-start.2 = (f32[2,2,32,512]{3,1,2,0:T(2,128)S(1)}, f32[2,2,32,512]{3,1,2,0:T(2,128)S(1)}, u32[]{:S(2)}, u32[]{:S(2)}) collective-permute-start(f32[2,2,32,512]{3,1,2,0:T(2,128)S(1)} %broadcast_select_fusion), channel_id=1, source_target_pairs={{64,0},{96,32},{128,64},{160,96},{192,128},{224,160},{256,192},{28... | collective-permute-start | bytes 786440 | tf_op jit(solution)/shard_map/ppermute | solution.py:14
  213.0 16.8 %collective-permute-start.3 = (f32[2,2,32,512]{3,1,2,0:T(2,128)S(1)}, f32[2,2,32,512]{3,1,2,0:T(2,128)S(1)}, u32[]{:S(2)}, u32[]{:S(2)}) collective-permute-start(f32[2,2,32,512]{3,1,2,0:T(2,128)S(1)} %broadcast_select_fusion.1), channel_id=1, source_target_pairs={{128,0},{160,32},{192,64},{224,96},{256,128},{288,160},{320,192},{... | collective-permute-start | bytes 786440 | tf_op jit(solution)/shard_map/ppermute | solution.py:14
  229.8 32.2 %copy-start.13 = (s32[4]{0:T(128)S(1)}, s32[4]{0:T(128)}, u32[]{:S(2)}) copy-start(s32[4]{0:T(128)} %constant.513) | copy-start | bytes 52
  230.0 9.8 %collective-permute-start.4 = (f32[2,2,32,512]{3,1,2,0:T(2,128)S(1)}, f32[2,2,32,512]{3,1,2,0:T(2,128)S(1)}, u32[]{:S(2)}, u32[]{:S(2)}) collective-permute-start(f32[2,2,32,512]{3,1,2,0:T(2,128)S(1)} %broadcast_select_fusion.2), channel_id=1, source_target_pairs={{256,0},{288,32},{320,64},{352,96},{384,128},{416,160},{448,192},{... | collective-permute-start | bytes 786440 | tf_op jit(solution)/shard_map/ppermute | solution.py:14
  240.9 16.2 %all-to-all-start.5 = ((f32[32,1,1024]{2,1,0:T(1,128)}), f32[32,1,1024]{2,1,0:T(1,128)S(1)}, u32[]{:S(2)}, u32[]{:S(2)}) async-start(f32[32,1,1024]{2,1,0:T(1,128)} %all_to_all.54), calls=%async_computation.5 | async-start | bytes 262144 | tf_op jit(solution)/shard_map/all_to_all | solution.py:24
  257.9 27.1 %all-to-all-start.6 = ((f32[32,1,1024]{2,1,0:T(1,128)}), f32[32,1,1024]{2,1,0:T(1,128)S(1)}, u32[]{:S(2)}, u32[]{:S(2)}) async-start(f32[32,1,1024]{2,1,0:T(1,128)} %broadcast_in_dim.192), calls=%async_computation.6 | async-start | bytes 262144 | tf_op jit(solution)/shard_map/all_to_all | solution.py:20
  285.1 37.9 %all-to-all-start.4 = ((f32[32,1,8192]{2,1,0:T(1,128)}), f32[32,1,8192]{2,1,0:T(1,128)S(1)}, u32[]{:S(2)}, u32[]{:S(2)}) async-start(f32[32,1,8192]{2,1,0:T(1,128)} %reshape.568), calls=%async_computation.4 | async-start | bytes 2097152 | tf_op jit(solution)/shard_map/all_to_all | solution.py:145
  (15 other events, 73.4 us)
